TPU v7x, 128 devices: a whole 4x4x4 slice. The times are simulated.
128 devices in a mesh: seq: 16 (over x_hi, z, core), kvh: 8 (over x_lo, y).
Axes of the slice: x: 4 (x_hi: 2, x_lo: 2; x = x_hi * 2 + x_lo), y: 4, z: 4, core: 2. Of those that a mesh axis runs over, the one named last changes fastest.
Arguments:
- normed: bfloat16 [4096, 4096], P('seq'), may hold values from -8 to 8
- w_query: bfloat16 [4096, 4096], P(None, 'kvh'), may hold values from -1 to 1, as said below
- w_key: bfloat16 [4096, 1024], P(None, 'kvh'), may hold values from -1 to 1, as said below
- w_value: bfloat16 [4096, 1024], P(None, 'kvh'), may hold values from -0.09375 to 0.09375
- positions: int32 [4096], P('seq'), may hold values from 0 to 4222, as said below
- block_mask: int32 [32, 32], P('seq'), may hold values from 0 to 1, as said below
- grad_attn: bfloat16 [4096, 4096], P('seq', 'kvh'), may hold values from -6 to 6
Outputs:
- grad_normed: bfloat16 [4096, 4096], P('seq', 'kvh')
- grad_wq: float32 [4096, 4096], P('seq', 'kvh')
- grad_wk: float32 [4096, 1024], P('seq', 'kvh')
- grad_wv: float32 [4096, 1024], P('seq', 'kvh')
Inputs may be any that keep to these rules, and one draw needn't show every extreme that they name: Within a block positions rise by one per token; block b starts between b * 128 and (b + 1) * 128 - 1, block 0 at 0, the last block at its latest start. `block_mask`: the diagonal is 1; a block may read only blocks of earlier rounds besides itself; entries for earlier rounds are 0 or 1. `w_query`: entries of about 4096^(-1/2) in size. `w_key`: entries of about 4096^(-1/2) in size.
All inputs are finite; a program needn't handle non-finite values.
Results may differ from a plain program's by a relative error of at most 0.019.
The roundings to bfloat16 on the way count: a program that leaves them out, or rounds other values in their place, can miss the bound.
Values may be sent and summed in bfloat16 or wider, within the bound.
No kernel may reach another device: no remote copies, remote signals or barrier semaphores. Data moves between devices by JAX's collectives and lax.ppermute only.
A program may use at most 128 MiB of HBM per device.

v0:
```python
import jax
import jax.numpy as jnp
from jax import lax
from jax.sharding import PartitionSpec as P

HEAD = 128
BLOCK = 128


THETA = 500000.0


def rotate(values, positions, rotation_sign):
    tok_rows = values.shape[0]
    head_count = values.shape[1] // HEAD
    half_size = HEAD // 2
    pieces = values.reshape(tok_rows, head_count, HEAD)
    frequency = THETA ** (-(jnp.arange(half_size, dtype=jnp.float32) * (2.0 / HEAD)))
    angles = positions.astype(jnp.float32)[:, None] * frequency[None, :]
    cosine = jnp.cos(angles)[:, None, :]
    sine_part = rotation_sign * jnp.sin(angles)[:, None, :]
    lower_half = pieces[:, :, :half_size]
    upper_half = pieces[:, :, half_size:]
    turned = jnp.concatenate(
        [
            lower_half * cosine - upper_half * sine_part,
            upper_half * cosine + lower_half * sine_part,
        ],
        axis=2,
    )
    return turned.reshape(tok_rows, head_count * HEAD)


def visible(mask_rows, query_block0, query_count, chunk_blocks, key_inner):
    query_local = jnp.arange(query_count)
    query_block = query_block0 + query_local // BLOCK
    table = jnp.take(mask_rows, chunk_blocks, axis=1) == 1
    key_blocks = jnp.repeat(chunk_blocks, BLOCK)
    allowed = jnp.repeat(jnp.repeat(table, BLOCK, axis=0), BLOCK, axis=1)
    inner_ok = key_inner[None, :] <= (query_local % BLOCK)[:, None]
    return allowed & ((query_block[:, None] != key_blocks[None, :]) | inner_ok)


def product(form, left, right):
    return jnp.einsum(form, left, right, preferred_element_type=jnp.float32)


def masked_scores(queries, keys, seen):
    scores = product("tgd,sd->gts", queries, keys) * HEAD ** (-0.5)
    return jnp.where(seen[None], scores, -1e30)


def softmax_stats(queries, keys, values, grad_heads, seen):
    scores = masked_scores(queries, keys, seen)
    row_max = jnp.max(scores, axis=2, keepdims=True)
    log_total = row_max[:, :, 0] + jnp.log(jnp.sum(jnp.exp(scores - row_max), axis=2))
    weights = jnp.where(seen[None], jnp.exp(scores - log_total[:, :, None]), 0.0).astype(
        jnp.bfloat16
    )
    outputs = product("gts,sd->gtd", weights, values)
    row_dots = jnp.sum(outputs * jnp.transpose(grad_heads.astype(jnp.float32), (1, 0, 2)), axis=2)
    return (log_total, row_dots)


def attention_grads(queries, keys, values, grad_heads, seen, log_total, row_dots):
    scores = masked_scores(queries, keys, seen)
    probs = jnp.where(seen[None], jnp.exp(scores - log_total[:, :, None]), 0.0)
    weights = probs.astype(jnp.bfloat16)
    grad_probs = product("tgd,sd->gts", grad_heads, values)
    grad_scores = (probs * (grad_probs - row_dots[:, :, None]) * HEAD ** (-0.5)).astype(
        jnp.bfloat16
    )
    grad_query = product("gts,sd->tgd", grad_scores, keys)
    grad_key = product("gts,tgd->sd", grad_scores, queries)
    grad_value = product("gts,tgd->sd", weights, grad_heads)
    return (grad_query, grad_key, grad_value)


SEQ_AXES = ("seq_x", "seq_z", "seq_core")
KVH_AXES = ("kvh_x", "kvh_y")
PAIR = [(0, 1), (1, 0)]


def seq_position():
    return (lax.axis_index("seq_x") * lax.axis_size("seq_z") + lax.axis_index("seq_z")) * 2 + lax.axis_index(
        "seq_core"
    )


def gather_rows(block):
    chips = lax.axis_size("seq_x") * lax.axis_size("seq_z")
    copies = jnp.broadcast_to(block[None], (chips,) + block.shape)
    mine = lax.all_to_all(copies, ("seq_x", "seq_z"), 0, 0, tiled=True)
    other = lax.ppermute(mine, "seq_core", PAIR)
    joined = jnp.stack([mine, other], axis=0)
    return joined.reshape((2 * chips * block.shape[0],) + block.shape[1:])


def pair_sum(keep, send):
    got = lax.ppermute(send.astype(jnp.bfloat16), "seq_core", PAIR)
    return (keep.astype(jnp.float32) + got.astype(jnp.float32)).astype(jnp.bfloat16)


def scatter_sum(parts, axis):
    arrived = lax.all_to_all(parts, axis, 0, 0, tiled=True)
    return jnp.sum(arrived.astype(jnp.float32), axis=0)


def body(normed, w_query, w_key, w_value, positions, block_mask, grad_attn):
    tok_rows = normed.shape[0]
    group_size = w_query.shape[1] // w_key.shape[1]
    width_query = group_size * HEAD
    blk_local = tok_rows // BLOCK
    chips = lax.axis_size("seq_x") * lax.axis_size("seq_z")
    kvh_count = lax.axis_size("kvh_x") * lax.axis_size("kvh_y")
    core = lax.axis_index("seq_core")
    my_index = seq_position()
    queries = rotate(
        jnp.dot(normed, w_query, preferred_element_type=jnp.float32), positions, 1.0
    ).astype(jnp.bfloat16)
    keys = rotate(
        jnp.dot(normed, w_key, preferred_element_type=jnp.float32), positions, 1.0
    ).astype(jnp.bfloat16)
    values = jnp.dot(normed, w_value, preferred_element_type=jnp.float32).astype(jnp.bfloat16)
    kv_all = gather_rows(jnp.concatenate([keys, values], axis=1))
    rounds = chips // 2
    chip_me = lax.axis_index("seq_x") * lax.axis_size("seq_z") + lax.axis_index("seq_z")
    round_me = chip_me // 2
    kv_grid = kv_all.reshape(2, rounds, 2, tok_rows, 2 * HEAD)
    own_kv = lax.dynamic_index_in_dim(
        lax.dynamic_index_in_dim(kv_grid[0], round_me, 0, keepdims=False), chip_me % 2, 0, keepdims=False
    )
    later = jnp.roll(kv_grid, -(round_me + 1), axis=1)[:, : rounds - 1]
    kv_sel = jnp.concatenate([own_kv[None], later.reshape(-1, tok_rows, 2 * HEAD)], axis=0)
    kv_sel = kv_sel.reshape(-1, 2 * HEAD)
    keys_all = kv_sel[:, :HEAD]
    values_all = kv_sel[:, HEAD:]
    key_count = keys_all.shape[0]
    per_shard = tok_rows // BLOCK
    chunk = jnp.arange(key_count // BLOCK - per_shard)
    shard = chunk // per_shard
    side = shard // (2 * (rounds - 1))
    chip = ((round_me + 1 + (shard // 2) % (rounds - 1)) % rounds) * 2 + shard % 2
    source = chip * 2 + jnp.where(side == 0, core, 1 - core)
    chunk_blocks = jnp.concatenate(
        [my_index * per_shard + jnp.arange(per_shard), source * per_shard + chunk % per_shard]
    )
    seen = visible(block_mask, my_index * blk_local, tok_rows, chunk_blocks, jnp.arange(key_count) % BLOCK)
    query_heads = queries.reshape(tok_rows, group_size, HEAD)
    grad_heads = grad_attn.reshape(tok_rows, group_size, HEAD)
    log_total, row_dots = softmax_stats(query_heads, keys_all, values_all, grad_heads, seen)
    grad_query, grad_key, grad_value = attention_grads(
        query_heads, keys_all, values_all, grad_heads, seen, log_total, row_dots
    )
    query_grad = rotate(grad_query.reshape(tok_rows, width_query), positions, -1.0).astype(
        jnp.bfloat16
    )
    kv_sel_terms = (
        jnp.concatenate([grad_key, grad_value], axis=1).astype(jnp.bfloat16).reshape(-1, tok_rows, 2 * HEAD)
    )
    later_terms = kv_sel_terms[1:].reshape(2, rounds - 1, 2, tok_rows, 2 * HEAD)
    place = (jnp.arange(2)[:, None] == 0) & (jnp.arange(2)[None, :] == chip_me % 2)
    own_round = jnp.where(place[:, :, None, None], kv_sel_terms[0][None, None], jnp.zeros((), jnp.bfloat16))
    kv_grid_terms = jnp.concatenate([later_terms, own_round[:, None]], axis=1)
    kv_grid_terms = jnp.roll(kv_grid_terms, round_me + 1, axis=1)
    kv_terms = kv_grid_terms.reshape(2, chips, tok_rows, 2 * HEAD)
    feat_split = normed.reshape(tok_rows, chips, 2, normed.shape[1] // (2 * chips))
    normed_even = feat_split[:, :, 0, :]
    normed_odd = feat_split[:, :, 1, :]
    tokens_first = (((0,), (0,)), ((), ()))
    first = core == 0

    def weight_halves(grads):
        even = lax.dot_general(normed_even, grads, tokens_first, preferred_element_type=jnp.float32)
        odd = lax.dot_general(normed_odd, grads, tokens_first, preferred_element_type=jnp.float32)
        return jnp.where(first, even, odd), jnp.where(first, odd, even)

    wq_keep, wq_send = weight_halves(query_grad)
    joint = pair_sum(
        jnp.concatenate([kv_terms[0], wq_keep], axis=2), jnp.concatenate([kv_terms[1], wq_send], axis=2)
    )
    joint_total = scatter_sum(joint, ("seq_x", "seq_z"))
    kv_total = joint_total[:, : 2 * HEAD]
    grad_wq = joint_total[:, 2 * HEAD :]

    def weight_terms(grads):
        keep, send = weight_halves(grads)
        return scatter_sum(pair_sum(keep, send), ("seq_x", "seq_z"))

    contract = (((1,), (1,)), ((), ()))
    partial_input = lax.dot_general(
        w_query, query_grad, contract, preferred_element_type=jnp.float32
    )
    key_grad = rotate(kv_total[:, :HEAD], positions, -1.0).astype(jnp.bfloat16)
    value_grad = kv_total[:, HEAD:].astype(jnp.bfloat16)
    kv_grad = jnp.concatenate([key_grad, value_grad], axis=1)
    grad_wkv = weight_terms(kv_grad)
    grad_wk = grad_wkv[:, :HEAD]
    grad_wv = grad_wkv[:, HEAD:]
    partial_input = partial_input + lax.dot_general(
        w_key, key_grad, contract, preferred_element_type=jnp.float32
    )
    partial_input = partial_input + lax.dot_general(
        w_value, value_grad, contract, preferred_element_type=jnp.float32
    )
    feat = partial_input.shape[0] // kvh_count
    input_terms = partial_input.astype(jnp.bfloat16).reshape(kvh_count, feat, tok_rows)
    grad_normed = scatter_sum(input_terms, KVH_AXES).T.astype(jnp.bfloat16)
    return (grad_normed, grad_wq, grad_wk, grad_wv)


def solution(mesh):
    seq_x = 2
    seq_size = mesh.shape["seq"]
    kvh_size = mesh.shape["kvh"]
    grid = mesh.devices.reshape(seq_x, seq_size // (2 * seq_x), 2, 2, kvh_size // 2)
    fine = jax.sharding.Mesh(grid, SEQ_AXES + KVH_AXES)
    in_specs = (
        P(SEQ_AXES, None),
        P(None, KVH_AXES),
        P(None, KVH_AXES),
        P(None, KVH_AXES),
        P(SEQ_AXES),
        P(SEQ_AXES, None),
        P(SEQ_AXES, KVH_AXES),
    )
    out_specs = (P(SEQ_AXES, KVH_AXES),) * 4
    return jax.shard_map(body, mesh=fine, in_specs=in_specs, out_specs=out_specs, check_vma=False)
```

profile of v0, /device:TPU:0, one launch (start us, length us, event | category | flops | bytes accessed | tf_op | source)
XLA Modules:
  0.0 195.0 jit_solution(2265453363644876510)
XLA Ops:
  0.7 0.8 convert_element_type.92
  1.5 2.8 %convolution_convert_fusion = bf16[256,128]{0,1:T(8,128)(2,1)S(1)} fusion(bf16[256,4096]{1,0:T(8,128)(2,1)} %param.9, bf16[4096,128]{1,0:T(8,128)(2,1)} %param.12), kind=kOutput, calls=%fused_computation.51 | convolution fusion | flops 268468224 | bytes 3211264 | tf_op jit(solution)/shard_map/dot_general | solution.py:124
  5.6 1.0 broadcast_in_dim.111
  6.7 8.0 %all-to-all-start = ((bf16[8,256,256]{2,1,0:T(8,128)(2,1)}), bf16[8,256,256]{2,1,0:T(8,128)(2,1)}, u32[]{:S(2)}, u32[]{:S(2)}) async-start(bf16[8,256,256]{2,1,0:T(8,128)(2,1)} %broadcast_in_dim.111), calls=%async_computation | async-start | bytes 2097152 | tf_op jit(solution)/shard_map/all_to_all | solution.py:93
  14.7 2.5 %copy.90 = bf16[256,4096]{0,1:T(8,128)(2,1)} copy(bf16[256,4096]{1,0:T(8,128)(2,1)S(1)} %copy-done.1) | data formatting | bytes 4194304 | tf_op args[0]
  18.3 0.8 copy.77
  19.1 4.2 %fusion.69 = f32[256,512]{1,0:T(8,128)} fusion(bf16[256,4096]{1,0:T(8,128)(2,1)S(1)} %copy-done.1, bf16[4096,512]{1,0:T(8,128)(2,1)} %param.10), kind=kOutput, calls=%fused_computation.163 | convolution fusion | flops 1073741824 | bytes 6815744 | tf_op jit(solution)/shard_map/dot_general | solution.py:119
  23.4 1.2 reshape.437
  24.7 1.9 bitcast_and_fusion
  26.5 4.0 %all-to-all-done = bf16[8,256,256]{2,1,0:T(8,128)(2,1)} async-done(((bf16[8,256,256]{2,1,0:T(8,128)(2,1)}), bf16[8,256,256]{2,1,0:T(8,128)(2,1)}, u32[]{:S(2)}, u32[]{:S(2)}) %all-to-all-start) | async-done | bytes 1048608 | tf_op jit(solution)/shard_map/all_to_all | solution.py:93
  31.7 0.9 dynamic-slice_bitcast_fusion
  32.6 0.8 collective-permute-done
  33.5 2.0 %fusion.15 = bf16[2,3,2,256,256]{4,3,2,1,0:T(8,128)(2,1)S(1)} fusion(s32[]{:T(128)S(6)} %select_n.306, bf16[1,4,2,256,256]{4,3,2,1,0:T(8,128)(2,1)} %bitcast.4, bf16[1,4,2,256,256]{4,3,2,1,0:T(8,128)(2,1)S(1)} %bitcast.142), kind=kLoop, calls=%fused_computation.45 | loop fusion | flops 2359296 | bytes 3670020 | tf_op jit(solution)/shard_map/jit(_roll_dynamic)/concatenate | solution.py:133
  35.6 2.4 %fusion.67 = (f32[4,256]{1,0:T(4,128)S(1)}, f32[4,256,3328]{1,2,0:T(8,128)S(1)}) fusion(bf16[256,4,64]{2,0,1:T(8,128)(2,1)S(1)} %get-tuple-element.26, bf16[256,4,64]{2,0,1:T(8,128)(2,1)S(1)} %get-tuple-element.25, bf16[3328,256]{1,0:T(8,128)(2,1)S(1)} %bitcast.138, pred[256,3328]{0,1:T(8,128)(4,1)S(1)} %copy-done.11), kind=kOutput, calls=%fused_computation.161 | convolution fusion | flops 883162112 | bytes 15863808 | tf_op jit(solution)/shard_map/tgd,sd->gts/dot_general | solution.py:45
  38.1 1.8 exponential_reduce_fusion
  39.9 3.9 %fusion.17 = f32[4,256]{1,0:T(4,128)S(1)} fusion(bf16[3328,256]{1,0:T(8,128)(2,1)} %bitcast.139, f32[4,256,3328]{1,2,0:T(8,128)S(1)} %get-tuple-element.41, f32[4,256]{1,0:T(4,128)S(1)} %log_add_fusion, pred[256,3328]{0,1:T(8,128)(4,1)} %bitcast_and_fusion, bf16[256,4,128]{0,2,1:T(8,128)(2,1)S(1)} %bitcast.144), kind=kOutput, calls=%fused_computation.49 | convolution fusion | flops 883031040 | bytes 15605760 | tf_op jit(solution)/shard_map/gts,sd->gtd/dot_general | solution.py:45
  43.8 3.1 %fusion.7 = bf16[3328,128]{0,1:T(8,128)(2,1)S(1)} fusion(bf16[256,4,128]{0,2,1:T(8,128)(2,1)S(1)} %bitcast.145, f32[4,256,3328]{1,2,0:T(8,128)S(1)} %get-tuple-element.41, f32[4,256]{1,0:T(4,128)S(1)} %log_add_fusion, pred[256,3328]{0,1:T(8,128)(4,1)S(1)} %copy-done.12), kind=kOutput, calls=%fused_computation.18 | convolution fusion | flops 883064832 | bytes 15601664 | tf_op jit(solution)/shard_map/gts,tgd->sd/dot_general | solution.py:45
  46.9 5.4 %fusion.2 = bf16[4,256,3328]{1,2,0:T(8,128)(2,1)S(1)} fusion(f32[4,256,3328]{1,2,0:T(8,128)S(1)} %get-tuple-element.41, bf16[256,4,128]{0,2,1:T(8,128)(2,1)S(1)} %bitcast.146, f32[4,256]{1,0:T(4,128)S(1)} %fusion.17, f32[4,256]{1,0:T(4,128)S(1)} %log_add_fusion, pred[256,3328]{0,1:T(8,128)(4,1)} %bitcast_and_fusion, bf16[3328,256]{1,0:T(8,128)(2,1)S(1)} %bitcast.140), kind=kOutput, calls=%fused_computation.4 | convolution fusion | flops 892862464 | bytes 22421504 | tf_op jit(solution)/shard_map/tgd,sd->gts/dot_general | solution.py:45
  52.3 2.8 %convolution_bitcast_fusion.2 = f32[256,4,128]{2,0,1:T(8,128)S(1)} fusion(bf16[4,256,3328]{1,2,0:T(8,128)(2,1)S(1)} %fusion.2, bf16[3328,256]{1,0:T(8,128)(2,1)S(1)} %bitcast.141), kind=kOutput, calls=%fused_computation.48 | convolution fusion | flops 872415232 | bytes 8192000 | tf_op jit(solution)/shard_map/gts,sd->tgd/dot_general | solution.py:45
  55.0 2.4 %fusion.6 = bf16[3328,128]{0,1:T(8,128)(2,1)S(1)} fusion(bf16[4,256,3328]{1,2,0:T(8,128)(2,1)S(1)} %fusion.2, bf16[256,4,64]{2,0,1:T(8,128)(2,1)S(1)} %get-tuple-element.26, bf16[256,4,64]{2,0,1:T(8,128)(2,1)S(1)} %get-tuple-element.25), kind=kOutput, calls=%fused_computation.17 | convolution fusion | flops 873365504 | bytes 7929856 | tf_op jit(solution)/shard_map/gts,tgd->sd/dot_general | solution.py:45
  57.5 1.4 fusion.13
  59.2 0.9 maximum_convert_fusion
  60.0 1.1 copy.84
  61.1 2.7 %fusion.22 = f32[512,8,256]{2,0,1:T(8,128)} fusion(bf16[256,512,1]{0,1,2:T(8,128)(2,1)S(1)} %bitcast.135, bf16[256,8,2,256]{0,3,2,1:T(8,128)(2,1)S(1)} %bitcast.126), kind=kOutput, calls=%fused_computation.59 | convolution fusion | flops 536870912 | bytes 5505024 | tf_op jit(solution)/shard_map/dot_general | solution.py:175
  63.9 2.7 %fusion.20 = f32[512,8,256]{2,0,1:T(8,128)} fusion(bf16[256,512,1]{0,1,2:T(8,128)(2,1)S(1)} %bitcast.136, bf16[256,8,2,256]{0,3,2,1:T(8,128)(2,1)S(1)} %bitcast.127), kind=kOutput, calls=%fused_computation.57 | convolution fusion | flops 536870912 | bytes 5505024 | tf_op jit(solution)/shard_map/dot_general | solution.py:174
  66.6 2.6 %copy.88 = bf16[3072,256]{1,0:T(8,128)(2,1)} copy(bf16[3072,256]{0,1:T(8,128)(2,1)} %fusion.13) | data formatting | bytes 3145728 | tf_op jit(solution)/shard_map/slice | solution.py:161
  69.9 1.0 broadcast_select_fusion
  70.9 2.8 %fusion.10 = bf16[2,4,2,256,256]{4,3,2,1,0:T(8,128)(2,1)S(1)} fusion(s32[]{:T(128)S(6)} %select_n.308, bf16[2,3,2,256,256]{4,3,2,1,0:T(8,128)(2,1)} %bitcast.132, bf16[2,1,2,256,256]{4,3,2,1,0:T(8,128)(2,1)S(1)} %broadcast_select_fusion), kind=kLoop, calls=%fused_computation.33 | loop fusion | flops 3145728 | bytes 4194308 | tf_op jit(solution)/shard_map/jit(_roll_dynamic)/concatenate | solution.py:165
  73.7 1.5 fusion.64
  75.2 2.3 %copy.94 = bf16[8,256,256]{1,2,0:T(8,128)(2,1)} copy(bf16[8,256,256]{2,1,0:T(8,128)(2,1)} %bitcast.134) | data formatting | bytes 2097152 | tf_op jit(solution)/shard_map/convert_element_type | solution.py:180
  77.5 2.8 %fusion.8 = bf16[8,256,512]{1,2,0:T(8,128)(2,1)S(1)} fusion(f32[512,8,256]{2,0,1:T(8,128)} %fusion.22, f32[512,8,256]{2,0,1:T(8,128)} %fusion.20, pred[]{:T(512)S(6)} %eq.63), kind=kLoop, calls=%fused_computation.31 | loop fusion | flops 1048576 | bytes 10485761 | tf_op jit(solution)/shard_map/jit(_where)/select_n | solution.py:176
  80.3 2.0 %pad_maximum_fusion = bf16[8,256,768]{1,2,0:T(8,128)(2,1)} fusion(bf16[8,256,512]{1,2,0:T(8,128)(2,1)S(1)} %fusion.8, bf16[8,256,256]{1,2,0:T(8,128)(2,1)S(1)} %copy-done.7), kind=kLoop, calls=%fused_computation.30 | loop fusion | flops 6291456 | bytes 6291456 | tf_op jit(solution)/shard_map/concatenate | solution.py:180
  82.4 1.6 bitcast_convert_fusion
  84.0 2.9 %copy.93 = f32[8,256,256]{1,2,0:T(8,128)} copy(f32[8,256,256]{2,1,0:T(8,128)} %bitcast_convert_fusion) | data formatting | bytes 4194304 | tf_op jit(solution)/shard_map/convert_element_type | solution.py:180
  86.9 3.1 %select_bitcast_fusion = f32[8,256,512]{1,2,0:T(8,128)S(1)} fusion(f32[512,8,256]{2,0,1:T(8,128)} %fusion.20, f32[512,8,256]{2,0,1:T(8,128)} %fusion.22, pred[]{:T(512)S(6)} %eq.63), kind=kLoop, calls=%fused_computation.28 | loop fusion | flops 1048576 | bytes 12582913 | tf_op jit(solution)/shard_map/jit(_where)/select_n | solution.py:176
  90.0 2.9 %fusion.4 = bf16[8,256,768]{1,2,0:T(8,128)(2,1)S(1)} fusion(f32[8,256,512]{1,2,0:T(8,128)S(1)} %select_bitcast_fusion, f32[8,256,256]{1,2,0:T(8,128)S(1)} %copy-done.3, bf16[8,256,768]{1,2,0:T(8,128)(2,1)} %collective-permute-done.1), kind=kLoop, calls=%fused_computation.10 | loop fusion | flops 6291456 | bytes 12582912 | tf_op jit(solution)/shard_map/convert_element_type | solution.py:101
  92.9 44.0 %all_to_all.20 = bf16[8,256,768]{1,2,0:T(8,128)(2,1)S(1)} all-to-all(bf16[8,256,768]{1,2,0:T(8,128)(2,1)S(1)} %fusion.4), channel_id=1, replica_groups=mesh['seq_x'=2,'seq_z'=4,'seq_core'=2,'kvh_x'=2,'kvh_y'=4] {'seq_x','seq..., dimensions={0} | all-to-all | bytes 6291456 | tf_op jit(solution)/shard_map/all_to_all | solution.py:105
  138.5 1.3 copy-done.4
  139.8 1.3 convolution_add_fusion
  142.0 1.5 copy.121
  143.4 4.5 %all-to-all-start.2 = ((bf16[8,512,256]{1,2,0:T(8,128)(2,1)}), bf16[8,512,256]{1,2,0:T(8,128)(2,1)}, u32[]{:S(2)}, u32[]{:S(2)}) async-start(bf16[8,512,256]{1,2,0:T(8,128)(2,1)} %bitcast.131), calls=%async_computation.2 | async-start | bytes 4194304 | tf_op jit(solution)/shard_map/all_to_all | solution.py:105
  149.4 2.6 %collective-permute-done.2 = bf16[8,256,256]{1,2,0:T(8,128)(2,1)S(1)} collective-permute-done((bf16[8,256,256]{1,2,0:T(8,128)(2,1)S(1)}, bf16[8,256,256]{1,2,0:T(8,128)(2,1)S(1)}, u32[]{:S(2)}, u32[]{:S(2)}) %collective-permute-start.2) | collective-permute-done | bytes 1048608 | tf_op jit(solution)/shard_map/ppermute | solution.py:100
  152.1 1.4 fusion.12
  153.5 19.2 %all-to-all-done.2 = bf16[8,512,256]{1,2,0:T(8,128)(2,1)} async-done(((bf16[8,512,256]{1,2,0:T(8,128)(2,1)}), bf16[8,512,256]{1,2,0:T(8,128)(2,1)}, u32[]{:S(2)}, u32[]{:S(2)}) %all-to-all-start.2) | async-done | bytes 2097184 | tf_op jit(solution)/shard_map/all_to_all | solution.py:105
  172.7 4.9 %all-to-all-start.3 = ((bf16[8,256,256]{1,2,0:T(8,128)(2,1)}), bf16[8,256,256]{1,2,0:T(8,128)(2,1)S(1)}, u32[]{:S(2)}, u32[]{:S(2)}) async-start(bf16[8,256,256]{1,2,0:T(8,128)(2,1)} %fusion.12), calls=%async_computation.3 | async-start | bytes 2097152 | tf_op jit(solution)/shard_map/all_to_all | solution.py:105
  177.6 1.0 copy.96
  178.6 2.7 %reduce_sum.51 = bf16[512,256]{0,1:T(8,128)(2,1)} reduce(bf16[8,512,256]{1,2,0:T(8,128)(2,1)} %all-to-all-done.2, bf16[]{:T(256)} %constant.216.clone.1), dimensions={0}, to_apply=%region_4.6 | reduce | flops 917504 | bytes 2359298 | tf_op jit(solution)/shard_map/reduce_sum | solution.py:106
  181.3 12.0 %all-to-all-done.3 = bf16[8,256,256]{1,2,0:T(8,128)(2,1)S(1)} async-done(((bf16[8,256,256]{1,2,0:T(8,128)(2,1)}), bf16[8,256,256]{1,2,0:T(8,128)(2,1)S(1)}, u32[]{:S(2)}, u32[]{:S(2)}) %all-to-all-start.3) | async-done | bytes 1048608 | tf_op jit(solution)/shard_map/all_to_all | solution.py:105
  (83 shorter events, 10.3 us)
Async XLA Ops:
  0.6 3.7 %copy-start = (bf16[4096,128]{1,0:T(8,128)(2,1)S(1)}, bf16[4096,128]{1,0:T(8,128)(2,1)}, u32[]{:S(2)}) copy-start(bf16[4096,128]{1,0:T(8,128)(2,1)} %param.11) | copy-start | bytes 3145732
  0.6 3.7 %copy-start.1 = (bf16[256,4096]{1,0:T(8,128)(2,1)S(1)}, bf16[256,4096]{1,0:T(8,128)(2,1)}, u32[]{:S(2)}) copy-start(bf16[256,4096]{1,0:T(8,128)(2,1)} %param.9) | copy-start | bytes 6291460
  6.7 10.7 %copy-start.15 = (s32[2,32]{1,0:T(2,128)S(1)}, s32[2,32]{1,0:T(2,128)}, u32[]{:S(2)}) copy-start(s32[2,32]{1,0:T(2,128)} %param.14) | copy-start | bytes 772
  6.7 11.6 %copy-start.13 = (bf16[256,512]{1,0:T(8,128)(2,1)S(1)}, bf16[256,512]{1,0:T(8,128)(2,1)}, u32[]{:S(2)}) copy-start(bf16[256,512]{1,0:T(8,128)(2,1)} %param.15) | copy-start | bytes 786436
  6.7 23.9 %all-to-all-start = ((bf16[8,256,256]{2,1,0:T(8,128)(2,1)}), bf16[8,256,256]{2,1,0:T(8,128)(2,1)}, u32[]{:S(2)}, u32[]{:S(2)}) async-start(bf16[8,256,256]{2,1,0:T(8,128)(2,1)} %broadcast_in_dim.111), calls=%async_computation | async-start | bytes 2097152 | tf_op jit(solution)/shard_map/all_to_all | solution.py:93
  30.6 2.9 %collective-permute-start = (bf16[8,256,256]{2,1,0:T(8,128)(2,1)}, bf16[8,256,256]{2,1,0:T(8,128)(2,1)S(1)}, u32[]{:S(2)}, u32[]{:S(2)}) collective-permute-start(bf16[8,256,256]{2,1,0:T(8,128)(2,1)} %all-to-all-done), channel_id=1, source_target_pairs={{0,8},{8,0},{1,9},{9,1},{2,10},{10,2},{3,11},{11,3},{4,12},{12,4},... | collective-permute-start | bytes 3145736 | tf_op jit(solution)/shard_map/ppermute | solution.py:94
  33.5 2.2 %copy-start.11 = (pred[256,3328]{0,1:T(8,128)(4,1)S(1)}, pred[256,3328]{0,1:T(8,128)(4,1)}, u32[]{:S(2)}) copy-start(pred[256,3328]{0,1:T(8,128)(4,1)} %bitcast_and_fusion) | copy-start | bytes 2555908
  35.6 2.5 %copy-start.8 = (bf16[13,256,256]{2,1,0:T(8,128)(2,1)}, bf16[13,256,256]{2,1,0:T(8,128)(2,1)S(1)}, u32[]{:S(2)}) copy-start(bf16[13,256,256]{2,1,0:T(8,128)(2,1)S(1)} %pad_maximum_fusion.1) | copy-start | bytes 5111812
  38.1 1.8 copy-start.14
  39.9 3.9 %copy-start.12 = (pred[256,3328]{0,1:T(8,128)(4,1)S(1)}, pred[256,3328]{0,1:T(8,128)(4,1)}, u32[]{:S(2)}) copy-start(pred[256,3328]{0,1:T(8,128)(4,1)} %bitcast_and_fusion) | copy-start | bytes 2555908
  43.8 3.1 %copy-start.9 = (bf16[13,256,256]{2,1,0:T(8,128)(2,1)S(1)}, bf16[13,256,256]{2,1,0:T(8,128)(2,1)}, u32[]{:S(2)}) copy-start(bf16[13,256,256]{2,1,0:T(8,128)(2,1)} %copy-done.8) | copy-start | bytes 5111812
  57.5 3.6 %copy-start.2 = (bf16[256,4096]{0,1:T(8,128)(2,1)S(1)}, bf16[256,4096]{0,1:T(8,128)(2,1)}, u32[]{:S(2)}) copy-start(bf16[256,4096]{0,1:T(8,128)(2,1)} %copy.90) | copy-start | bytes 6291460
  77.5 2.8 %copy-start.7 = (bf16[8,256,256]{1,2,0:T(8,128)(2,1)S(1)}, bf16[8,256,256]{1,2,0:T(8,128)(2,1)}, u32[]{:S(2)}) copy-start(bf16[8,256,256]{1,2,0:T(8,128)(2,1)} %copy.94) | copy-start | bytes 3145732
  80.3 2.1 %copy-start.6 = (bf16[1,4,2,256,256]{4,3,2,1,0:T(8,128)(2,1)S(1)}, bf16[1,4,2,256,256]{4,3,2,1,0:T(8,128)(2,1)}, u32[]{:S(2)}) copy-start(bf16[1,4,2,256,256]{4,3,2,1,0:T(8,128)(2,1)} %get-tuple-element.24) | copy-start | bytes 3145732
  82.3 7.7 %collective-permute-start.1 = (bf16[8,256,768]{1,2,0:T(8,128)(2,1)}, bf16[8,256,768]{1,2,0:T(8,128)(2,1)}, u32[]{:S(2)}, u32[]{:S(2)}) collective-permute-start(bf16[8,256,768]{1,2,0:T(8,128)(2,1)} %pad_maximum_fusion), channel_id=1, source_target_pairs={{0,8},{8,0},{1,9},{9,1},{2,10},{10,2},{3,11},{11,3},{4,12},{12,4},... | collective-permute-start | bytes 9437192 | tf_op jit(solution)/shard_map/ppermute | solution.py:100
  86.9 3.1 %copy-start.3 = (f32[8,256,256]{1,2,0:T(8,128)S(1)}, f32[8,256,256]{1,2,0:T(8,128)}, u32[]{:S(2)}) copy-start(f32[8,256,256]{1,2,0:T(8,128)} %copy.93) | copy-start | bytes 6291460
  137.3 3.8 %copy-start.10 = (f32[256,768]{0,1:T(8,128)}, f32[256,768]{0,1:T(8,128)S(1)}, u32[]{:S(2)}) copy-start(f32[256,768]{0,1:T(8,128)S(1)} %convert_reduce_fusion) | copy-start | bytes 2359300
  137.4 2.5 %copy-start.4 = (bf16[4096,512]{1,0:T(8,128)(2,1)S(1)}, bf16[4096,512]{1,0:T(8,128)(2,1)}, u32[]{:S(2)}) copy-start(bf16[4096,512]{1,0:T(8,128)(2,1)} %param.10) | copy-start | bytes 12582916
  139.8 1.4 copy-start.5
  143.4 29.3 %all-to-all-start.2 = ((bf16[8,512,256]{1,2,0:T(8,128)(2,1)}), bf16[8,512,256]{1,2,0:T(8,128)(2,1)}, u32[]{:S(2)}, u32[]{:S(2)}) async-start(bf16[8,512,256]{1,2,0:T(8,128)(2,1)} %bitcast.131), calls=%async_computation.2 | async-start | bytes 4194304 | tf_op jit(solution)/shard_map/all_to_all | solution.py:105
  149.3 28.3 %slice-start = ((f32[256,768]{0,1:T(8,128)}), f32[256,512]{0,1:T(8,128)S(1)}, s32[]{:S(2)}) async-start(f32[256,768]{0,1:T(8,128)} %copy-done.10), calls=%async_computation.4 | async-start | bytes 1048576 | tf_op jit(solution)/shard_map/slice | solution.py:184
  149.3 2.7 %collective-permute-start.2 = (bf16[8,256,256]{1,2,0:T(8,128)(2,1)S(1)}, bf16[8,256,256]{1,2,0:T(8,128)(2,1)S(1)}, u32[]{:S(2)}, u32[]{:S(2)}) collective-permute-start(bf16[8,256,256]{1,2,0:T(8,128)(2,1)S(1)} %fusion.18), channel_id=1, source_target_pairs={{0,8},{8,0},{1,9},{9,1},{2,10},{10,2},{3,11},{11,3},{4,12},{12,4},... | collective-permute-start | bytes 3145736 | tf_op jit(solution)/shard_map/ppermute | solution.py:100
  172.7 20.6 %all-to-all-start.3 = ((bf16[8,256,256]{1,2,0:T(8,128)(2,1)}), bf16[8,256,256]{1,2,0:T(8,128)(2,1)S(1)}, u32[]{:S(2)}, u32[]{:S(2)}) async-start(bf16[8,256,256]{1,2,0:T(8,128)(2,1)} %fusion.12), calls=%async_computation.3 | async-start | bytes 2097152 | tf_op jit(solution)/shard_map/all_to_all | solution.py:105
where the time goes:
time: 196 us; the launch traced here: 195 us
  blocking collectives  44 us (22%)
  waiting for transfers between devices  38.8 us (20%)
  matrix products  36.9 us (19%)
  other arithmetic  32.1 us (16%)
  local copies, waits for them, and re-layouts  24.4 us (12%)
  starting transfers between devices  17.6 us (9%)
    all_to_all x1, blocking collectives, scatter_sum(): arrived = lax.all_to_all(parts, axis, 0, 0, tiled=True)  44 us
    all_to_all x2, waiting for transfers between devices, scatter_sum(): arrived = lax.all_to_all(parts, axis, 0, 0, tiled=True)  31.3 us
    dot_general x6, matrix products, product(): return jnp.einsum(form, left, right, preferred_element_type=jnp.float32)  19.9 us
    all_to_all x2, starting transfers between devices, scatter_sum(): arrived = lax.all_to_all(parts, axis, 0, 0, tiled=True)  9.42 us
    all_to_all x1, starting transfers between devices, gather_rows(): mine = lax.all_to_all(copies, ('seq_x', 'seq_z'), 0, 0, tiled=True)  7.99 us
    unnamed x41, local copies, waits for them, and re-layouts  7.48 us
    select_n x2, other arithmetic, weight_halves(): return (jnp.where(first, even, odd), jnp.where(first, odd, even))  5.85 us
    convert_element_type x2, other arithmetic, pair_sum(): (keep.astype(jnp.float32) + got.astype(jnp.float32)).astype(jnp.bfloat16)  4.34 us
  transfers between devices with their start and end apart: 6, of which 5 were waited for; matrix products, arithmetic and copies ran while one was open for 14% of the time, Pallas kernels for 0%

commit v1 on v0

--- a/solution.py
+++ b/solution.py
@@ -165,15 +165,14 @@
     kv_grid_terms = jnp.roll(kv_grid_terms, round_me + 1, axis=1)
     kv_terms = kv_grid_terms.reshape(2, chips, tok_rows, 2 * HEAD)
     feat_split = normed.reshape(tok_rows, chips, 2, normed.shape[1] // (2 * chips))
-    normed_even = feat_split[:, :, 0, :]
-    normed_odd = feat_split[:, :, 1, :]
+    by_core = jnp.transpose(feat_split, (0, 2, 1, 3))
+    normed_perm = jnp.where(core == 0, by_core, by_core[:, ::-1]).reshape(tok_rows, -1)
     tokens_first = (((0,), (0,)), ((), ()))
-    first = core == 0
 
     def weight_halves(grads):
-        even = lax.dot_general(normed_even, grads, tokens_first, preferred_element_type=jnp.float32)
-        odd = lax.dot_general(normed_odd, grads, tokens_first, preferred_element_type=jnp.float32)
-        return jnp.where(first, even, odd), jnp.where(first, odd, even)
+        full = lax.dot_general(normed_perm, grads, tokens_first, preferred_element_type=jnp.float32)
+        full = full.reshape((2, chips, -1) + grads.shape[1:])
+        return full[0], full[1]
 
     wq_keep, wq_send = weight_halves(query_grad)
     joint = pair_sum(

time: 196 us -> 203 us (1.036)
  matrix products: 36.9 us -> 41.3 us
  blocking collectives: 44 us -> 47.1 us
  other arithmetic: 32.1 us -> 29.4 us
    dot_general x6, matrix products: 19.9 us -> 28 us  [product(): return jnp.einsum(form, left, right, preferred_element_type=jnp.float32)]
    convert_element_type x2 -> x0, local copies, waits for them, and re-layouts: 5.16 us -> none  [the longest x1 2.88 us: body(): jnp.concatenate([kv_terms[0], wq_keep], axis=2)]
    reduce_sum x1, other arithmetic: 1.8 us -> 6.82 us  [softmax_stats(): jnp.sum(jnp.exp(scores - row_max), axis=2)]
    dot_general x4 -> x2, matrix products: 6.35 us -> 2.02 us  [weight_halves(): lax.dot_general(normed_perm, grads, tokens_first, preferred_element_type=...]
    ppermute x2, waiting for transfers between devices: 2.65 us -> 6.88 us  [pair_sum(): got = lax.ppermute(send.astype(jnp.bfloat16), 'seq_core', PAIR)]
    all_to_all x1, waiting for transfers between devices: 4.05 us -> 0.12 us  [gather_rows(): mine = lax.all_to_all(copies, ('seq_x', 'seq_z'), 0, 0, tiled=True)]
    all_to_all x1, blocking collectives: 44 us -> 47.1 us  [scatter_sum(): arrived = lax.all_to_all(parts, axis, 0, 0, tiled=True)]
    select_n x2 -> x1, other arithmetic: 5.85 us -> 2.89 us  [body(): jnp.where(core == 0, by_core, by_core[:, ::-1]).reshape(tok_rows, -1)]
  transfers between devices with their start and end apart: 6 -> 6, of which waited for: 5 -> 5; matrix products, arithmetic and copies ran while one was open for 14% -> 13% of each run, Pallas kernels for 0% -> 0%
where the time goes in v1:
time: 203 us; the launch traced here: 202 us
  blocking collectives  47.1 us (23%)
  matrix products  41.3 us (20%)
  waiting for transfers between devices  39 us (19%)
  other arithmetic  29.4 us (14%)
  local copies, waits for them, and re-layouts  26.1 us (13%)
  starting transfers between devices  18.1 us (9%)
    all_to_all x1, blocking collectives, scatter_sum(): arrived = lax.all_to_all(parts, axis, 0, 0, tiled=True)  47.1 us
    all_to_all x2, waiting for transfers between devices, scatter_sum(): arrived = lax.all_to_all(parts, axis, 0, 0, tiled=True)  32 us
    dot_general x6, matrix products, product(): return jnp.einsum(form, left, right, preferred_element_type=jnp.float32)  28 us
    all_to_all x2, starting transfers between devices, scatter_sum(): arrived = lax.all_to_all(parts, axis, 0, 0, tiled=True)  9.39 us
    unnamed x54, local copies, waits for them, and re-layouts  8.36 us
    all_to_all x1, starting transfers between devices, gather_rows(): mine = lax.all_to_all(copies, ('seq_x', 'seq_z'), 0, 0, tiled=True)  7.86 us
    ppermute x2, waiting for transfers between devices, pair_sum(): got = lax.ppermute(send.astype(jnp.bfloat16), 'seq_core', PAIR)  6.88 us
    reduce_sum x1, other arithmetic, softmax_stats(): jnp.sum(jnp.exp(scores - row_max), axis=2)  6.82 us
  transfers between devices with their start and end apart: 6, of which 5 were waited for; matrix products, arithmetic and copies ran while one was open for 13% of the time, Pallas kernels for 0%

profile of v1, /device:TPU:0, one launch (start us, length us, event | category | flops | bytes accessed | tf_op | source)
XLA Modules:
  0.0 202.3 jit_solution(16893470092658637586)
XLA Ops:
  0.7 0.8 convert_element_type.86
  1.9 2.4 %convolution_bitcast_fusion.3 = f32[256,1,128]{0,2,1:T(8,128)S(1)} fusion(bf16[256,4096]{1,0:T(8,128)(2,1)} %param.9, bf16[4096,128]{1,0:T(8,128)(2,1)S(1)} %copy-done), kind=kOutput, calls=%fused_computation.48 | convolution fusion | flops 268435456 | bytes 3276800 | tf_op jit(solution)/shard_map/dot_general | solution.py:122
  4.4 0.8 convolution_convert_fusion
  5.7 1.0 broadcast_in_dim.111
  6.7 7.9 %all-to-all-start = ((bf16[8,256,256]{2,1,0:T(8,128)(2,1)}), bf16[8,256,256]{2,1,0:T(8,128)(2,1)}, u32[]{:S(2)}, u32[]{:S(2)}) async-start(bf16[8,256,256]{2,1,0:T(8,128)(2,1)} %broadcast_in_dim.111), calls=%async_computation | async-start | bytes 2097152 | tf_op jit(solution)/shard_map/all_to_all | solution.py:93
  14.8 4.2 %fusion.64 = f32[256,512]{1,0:T(8,128)} fusion(bf16[256,4096]{1,0:T(8,128)(2,1)S(1)} %copy-done.1, bf16[4096,512]{1,0:T(8,128)(2,1)} %param.10), kind=kOutput, calls=%fused_computation.153 | convolution fusion | flops 1073741824 | bytes 6815744 | tf_op jit(solution)/shard_map/dot_general | solution.py:119
  20.0 2.5 %copy.105 = bf16[256,4096]{0,1:T(8,128)(2,1)} copy(bf16[256,4096]{1,0:T(8,128)(2,1)S(1)} %copy-done.1) | data formatting | bytes 4194304 | tf_op args[0]
  22.5 2.0 %reshape.447 = f32[256,4,128]{2,1,0:T(4,128)} reshape(f32[256,512]{1,0:T(8,128)} %fusion.64) | data formatting | bytes 1048576 | tf_op jit(solution)/shard_map/reshape | solution.py:17
  24.5 0.8 copy.92
  25.3 2.9 %reverse_select_fusion = bf16[256,2,8,256]{0,3,1,2:T(8,128)(2,1)S(1)} fusion(bf16[256,2,8,256]{0,3,1,2:T(8,128)(2,1)} %bitcast.114, pred[]{:T(512)S(6)} %eq.63), kind=kLoop, calls=%fused_computation.30 | loop fusion | flops 1048576 | bytes 4194305 | tf_op jit(solution)/shard_map/jit(_where)/select_n | solution.py:169
  28.5 1.9 bitcast_and_fusion
  31.3 1.6 fusion.61
  33.0 0.9 dynamic-slice_bitcast_fusion
  33.9 2.0 fusion.13
  36.1 6.2 %fusion.63 = (f32[4,256]{1,0:T(4,128)S(1)}, f32[4,256,3328]{1,2,0:T(8,128)}) fusion(bf16[256,4,64]{2,0,1:T(8,128)(2,1)S(1)} %get-tuple-element.22, bf16[256,4,64]{2,0,1:T(8,128)(2,1)S(1)} %get-tuple-element.21, bf16[3328,256]{1,0:T(8,128)(2,1)S(1)} %bitcast.119, pred[256,3328]{0,1:T(8,128)(4,1)S(1)} %copy-done.12), kind=kOutput, calls=%fused_computation.152 | convolution fusion | flops 883162112 | bytes 15863808 | tf_op jit(solution)/shard_map/tgd,sd->gts/dot_general | solution.py:45
  42.3 6.8 %exponential_reduce_fusion = f32[4,256]{1,0:T(4,128)S(1)} fusion(f32[4,256,3328]{1,2,0:T(8,128)} %get-tuple-element.37, f32[4,256]{1,0:T(4,128)S(1)} %get-tuple-element.36), kind=kLoop, calls=%fused_computation.7 | loop fusion | flops 6814720 | bytes 13639680 | tf_op jit(solution)/shard_map/reduce_sum | solution.py:56
  49.2 7.7 %fusion.7 = bf16[3328,128]{0,1:T(8,128)(2,1)S(1)} fusion(bf16[256,4,128]{0,2,1:T(8,128)(2,1)S(1)} %bitcast.129, f32[4,256,3328]{1,2,0:T(8,128)} %get-tuple-element.37, f32[4,256]{1,0:T(4,128)S(1)} %log_add_fusion, pred[256,3328]{0,1:T(8,128)(4,1)S(1)} %copy-done.12), kind=kOutput, calls=%fused_computation.18 | convolution fusion | flops 883064832 | bytes 15601664 | tf_op jit(solution)/shard_map/gts,tgd->sd/dot_general | solution.py:45
  57.0 2.3 %fusion.15 = f32[4,256]{1,0:T(4,128)S(1)} fusion(bf16[3328,256]{1,0:T(8,128)(2,1)S(1)} %bitcast.120, f32[4,256,3328]{1,2,0:T(8,128)S(1)} %bitcast.110, f32[4,256]{1,0:T(4,128)S(1)} %log_add_fusion, pred[256,3328]{0,1:T(8,128)(4,1)S(1)} %copy-done.12, bf16[256,4,128]{0,2,1:T(8,128)(2,1)S(1)} %bitcast.130), kind=kOutput, calls=%fused_computation.47 | convolution fusion | flops 883031040 | bytes 15605760 | tf_op jit(solution)/shard_map/gts,sd->gtd/dot_general | solution.py:45
  59.3 5.7 %fusion.2 = bf16[4,256,3328]{1,2,0:T(8,128)(2,1)S(1)} fusion(f32[4,256,3328]{1,2,0:T(8,128)S(1)} %bitcast.110, bf16[256,4,128]{0,2,1:T(8,128)(2,1)S(1)} %bitcast.131, f32[4,256]{1,0:T(4,128)S(1)} %fusion.15, f32[4,256]{1,0:T(4,128)S(1)} %log_add_fusion, pred[256,3328]{0,1:T(8,128)(4,1)} %bitcast_and_fusion, bf16[3328,256]{1,0:T(8,128)(2,1)} %bitcast.121), kind=kOutput, calls=%fused_computation.4 | convolution fusion | flops 892862464 | bytes 22421504 | tf_op jit(solution)/shard_map/tgd,sd->gts/dot_general | solution.py:45
  65.0 2.4 %fusion.6 = bf16[3328,128]{0,1:T(8,128)(2,1)S(1)} fusion(bf16[4,256,3328]{1,2,0:T(8,128)(2,1)S(1)} %fusion.2, bf16[256,4,64]{2,0,1:T(8,128)(2,1)S(1)} %get-tuple-element.22, bf16[256,4,64]{2,0,1:T(8,128)(2,1)S(1)} %get-tuple-element.21), kind=kOutput, calls=%fused_computation.17 | convolution fusion | flops 873365504 | bytes 7929856 | tf_op jit(solution)/shard_map/gts,tgd->sd/dot_general | solution.py:45
  67.5 1.4 fusion.11
  69.5 3.6 %convolution_bitcast_fusion.2 = f32[256,4,128]{2,0,1:T(8,128)} fusion(bf16[4,256,3328]{1,2,0:T(8,128)(2,1)S(1)} %fusion.2, bf16[3328,256]{1,0:T(8,128)(2,1)S(1)} %bitcast.122), kind=kOutput, calls=%fused_computation.46 | convolution fusion | flops 872415232 | bytes 8192000 | tf_op jit(solution)/shard_map/gts,sd->tgd/dot_general | solution.py:45
  73.1 0.8 copy.104
  73.9 2.6 %copy.103 = bf16[3072,256]{1,0:T(8,128)(2,1)} copy(bf16[3072,256]{0,1:T(8,128)(2,1)} %fusion.11) | data formatting | bytes 3145728 | tf_op jit(solution)/shard_map/slice | solution.py:161
  76.5 1.0 broadcast_select_fusion
  77.5 2.8 %fusion.9 = bf16[2,4,2,256,256]{4,3,2,1,0:T(8,128)(2,1)S(1)} fusion(s32[]{:T(128)S(6)} %select_n.275, bf16[2,3,2,256,256]{4,3,2,1,0:T(8,128)(2,1)} %bitcast.116, bf16[2,1,2,256,256]{4,3,2,1,0:T(8,128)(2,1)S(1)} %broadcast_select_fusion), kind=kLoop, calls=%fused_computation.32 | loop fusion | flops 3145728 | bytes 4194308 | tf_op jit(solution)/shard_map/jit(_roll_dynamic)/concatenate | solution.py:165
  80.3 1.5 fusion.60
  82.0 0.9 maximum_convert_fusion
  82.9 1.1 copy.99
  84.0 1.3 fusion.65
  85.6 0.9 copy-done.7
  88.2 4.4 %collective-permute-done.1 = bf16[8,256,768]{2,1,0:T(8,128)(2,1)S(1)} collective-permute-done((bf16[8,256,768]{2,1,0:T(8,128)(2,1)S(1)}, bf16[8,256,768]{2,1,0:T(8,128)(2,1)S(1)}, u32[]{:S(2)}, u32[]{:S(2)}) %collective-permute-start.1) | collective-permute-done | bytes 3145760 | tf_op jit(solution)/shard_map/ppermute | solution.py:100
  92.6 1.1 fusion.4
  93.7 47.1 %all_to_all.20 = bf16[8,256,768]{2,1,0:T(8,128)(2,1)S(1)} all-to-all(bf16[8,256,768]{2,1,0:T(8,128)(2,1)S(1)} %fusion.4), channel_id=1, replica_groups=mesh['seq_x'=2,'seq_z'=4,'seq_core'=2,'kvh_x'=2,'kvh_y'=4] {'seq_x','seq..., dimensions={0} | all-to-all | bytes 6291456 | tf_op jit(solution)/shard_map/all_to_all | solution.py:105
  142.8 1.0 copy.123
  143.8 1.0 fusion.32
  144.8 0.9 copy.124
  145.8 1.7 fusion.59
  148.0 1.3 convolution_add_fusion
  150.1 1.5 copy.132
  151.6 4.5 %all-to-all-start.2 = ((bf16[8,512,256]{1,2,0:T(8,128)(2,1)}), bf16[8,512,256]{1,2,0:T(8,128)(2,1)}, u32[]{:S(2)}, u32[]{:S(2)}) async-start(bf16[8,512,256]{1,2,0:T(8,128)(2,1)} %bitcast.113), calls=%async_computation.2 | async-start | bytes 4194304 | tf_op jit(solution)/shard_map/all_to_all | solution.py:105
  157.2 2.5 %collective-permute-done.2 = bf16[8,256,256]{2,1,0:T(8,128)(2,1)S(1)} collective-permute-done((bf16[8,256,256]{2,1,0:T(8,128)(2,1)S(1)}, bf16[8,256,256]{2,1,0:T(8,128)(2,1)S(1)}, u32[]{:S(2)}, u32[]{:S(2)}) %collective-permute-start.2) | collective-permute-done | bytes 1048608 | tf_op jit(solution)/shard_map/ppermute | solution.py:100
  159.7 1.3 add_convert_fusion
  161.0 19.9 %all-to-all-done.2 = bf16[8,512,256]{1,2,0:T(8,128)(2,1)} async-done(((bf16[8,512,256]{1,2,0:T(8,128)(2,1)}), bf16[8,512,256]{1,2,0:T(8,128)(2,1)}, u32[]{:S(2)}, u32[]{:S(2)}) %all-to-all-start.2) | async-done | bytes 2097184 | tf_op jit(solution)/shard_map/all_to_all | solution.py:105
  180.9 4.9 %all-to-all-start.3 = ((bf16[8,256,256]{2,1,0:T(8,128)(2,1)}), bf16[8,256,256]{2,1,0:T(8,128)(2,1)S(1)}, u32[]{:S(2)}, u32[]{:S(2)}) async-start(bf16[8,256,256]{2,1,0:T(8,128)(2,1)} %add_convert_fusion), calls=%async_computation.3 | async-start | bytes 2097152 | tf_op jit(solution)/shard_map/all_to_all | solution.py:105
  185.8 0.9 slice.132
  186.6 2.7 %reduce_sum.51 = bf16[512,256]{0,1:T(8,128)(2,1)} reduce(bf16[8,512,256]{1,2,0:T(8,128)(2,1)} %all-to-all-done.2, bf16[]{:T(256)} %constant.216.clone.1), dimensions={0}, to_apply=%region_4.6 | reduce | flops 917504 | bytes 2359298 | tf_op jit(solution)/shard_map/reduce_sum | solution.py:106
  189.3 12.2 %all-to-all-done.3 = bf16[8,256,256]{2,1,0:T(8,128)(2,1)S(1)} async-done(((bf16[8,256,256]{2,1,0:T(8,128)(2,1)}), bf16[8,256,256]{2,1,0:T(8,128)(2,1)S(1)}, u32[]{:S(2)}, u32[]{:S(2)}) %all-to-all-start.3) | async-done | bytes 1048608 | tf_op jit(solution)/shard_map/all_to_all | solution.py:105
  (95 shorter events, 11.4 us)
Async XLA Ops:
  0.6 1.2 copy-start
  0.6 3.7 %copy-start.1 = (bf16[256,4096]{1,0:T(8,128)(2,1)S(1)}, bf16[256,4096]{1,0:T(8,128)(2,1)}, u32[]{:S(2)}) copy-start(bf16[256,4096]{1,0:T(8,128)(2,1)} %param.9) | copy-start | bytes 6291460
  0.7 3.7 %copy-start.4 = (bf16[4096,128]{1,0:T(8,128)(2,1)S(1)}, bf16[4096,128]{1,0:T(8,128)(2,1)}, u32[]{:S(2)}) copy-start(bf16[4096,128]{1,0:T(8,128)(2,1)} %param.12) | copy-start | bytes 3145732
  4.4 10.4 %copy-start.18 = (s32[2,32]{1,0:T(2,128)S(1)}, s32[2,32]{1,0:T(2,128)}, u32[]{:S(2)}) copy-start(s32[2,32]{1,0:T(2,128)} %param.14) | copy-start | bytes 772
  6.7 23.8 %all-to-all-start = ((bf16[8,256,256]{2,1,0:T(8,128)(2,1)}), bf16[8,256,256]{2,1,0:T(8,128)(2,1)}, u32[]{:S(2)}, u32[]{:S(2)}) async-start(bf16[8,256,256]{2,1,0:T(8,128)(2,1)} %broadcast_in_dim.111), calls=%async_computation | async-start | bytes 2097152 | tf_op jit(solution)/shard_map/all_to_all | solution.py:93
  19.1 5.4 %copy-start.15 = (bf16[256,512]{1,0:T(8,128)(2,1)S(1)}, bf16[256,512]{1,0:T(8,128)(2,1)}, u32[]{:S(2)}) copy-start(bf16[256,512]{1,0:T(8,128)(2,1)} %param.15) | copy-start | bytes 786436
  30.5 3.4 %collective-permute-start = (bf16[8,256,256]{2,1,0:T(8,128)(2,1)}, bf16[8,256,256]{2,1,0:T(8,128)(2,1)S(1)}, u32[]{:S(2)}, u32[]{:S(2)}) collective-permute-start(bf16[8,256,256]{2,1,0:T(8,128)(2,1)} %all-to-all-done), channel_id=1, source_target_pairs={{0,8},{8,0},{1,9},{9,1},{2,10},{10,2},{3,11},{11,3},{4,12},{12,4},... | collective-permute-start | bytes 3145736 | tf_op jit(solution)/shard_map/ppermute | solution.py:94
  33.9 2.2 %copy-start.12 = (pred[256,3328]{0,1:T(8,128)(4,1)S(1)}, pred[256,3328]{0,1:T(8,128)(4,1)}, u32[]{:S(2)}) copy-start(pred[256,3328]{0,1:T(8,128)(4,1)} %bitcast_and_fusion) | copy-start | bytes 2555908
  36.1 20.8 %copy-start.8 = (bf16[13,256,256]{2,1,0:T(8,128)(2,1)}, bf16[13,256,256]{2,1,0:T(8,128)(2,1)S(1)}, u32[]{:S(2)}) copy-start(bf16[13,256,256]{2,1,0:T(8,128)(2,1)S(1)} %pad_maximum_fusion.1) | copy-start | bytes 5111812
  42.3 6.8 %copy-start.16 = (bf16[256,512]{0,1:T(8,128)(2,1)S(1)}, bf16[256,512]{0,1:T(8,128)(2,1)}, u32[]{:S(2)}) copy-start(bf16[256,512]{0,1:T(8,128)(2,1)} %copy.92) | copy-start | bytes 786436
  42.3 14.6 %slice-start = ((s8[13631488]{0:T(1024)(128)(4,1)}), s8[4194304]{0:T(1024)(128)(4,1)S(1)}, s32[]{:S(2)}) async-start(s8[13631488]{0:T(1024)(128)(4,1)} %bitcast.109), calls=%async_computation.4 | async-start | bytes 8388608
  42.3 14.6 %slice-start.1 = ((s8[13631488]{0:T(1024)(128)(4,1)}), s8[1048576]{0:T(1024)(128)(4,1)S(1)}, s32[]{:S(2)}) async-start(s8[13631488]{0:T(1024)(128)(4,1)} %bitcast.109), calls=%async_computation.5 | async-start | bytes 2097152
  49.1 7.8 %slice-start.2 = ((s8[13631488]{0:T(1024)(128)(4,1)}), s8[4194304]{0:T(1024)(128)(4,1)S(1)}, s32[]{:S(2)}) async-start(s8[13631488]{0:T(1024)(128)(4,1)} %bitcast.109), calls=%async_computation.6 | async-start | bytes 8388608
  49.2 7.8 %slice-start.3 = ((s8[13631488]{0:T(1024)(128)(4,1)}), s8[4194304]{0:T(1024)(128)(4,1)S(1)}, s32[]{:S(2)}) async-start(s8[13631488]{0:T(1024)(128)(4,1)} %bitcast.109), calls=%async_computation.7 | async-start | bytes 8388608
  57.0 2.4 %copy-start.17 = (bf16[256,512]{0,1:T(8,128)(2,1)S(1)}, bf16[256,512]{0,1:T(8,128)(2,1)}, u32[]{:S(2)}) copy-start(bf16[256,512]{0,1:T(8,128)(2,1)} %copy.92) | copy-start | bytes 786436
  67.5 2.0 copy-start.9
  77.5 4.3 %copy-start.2 = (f32[256,4,128]{2,0,1:T(8,128)S(1)}, f32[256,4,128]{2,0,1:T(8,128)}, u32[]{:S(2)}) copy-start(f32[256,4,128]{2,0,1:T(8,128)} %convolution_bitcast_fusion.2) | copy-start | bytes 1572868
  85.3 1.2 copy-start.7
  86.7 1.2 copy-start.6
  86.7 5.9 %collective-permute-start.1 = (bf16[8,256,768]{2,1,0:T(8,128)(2,1)S(1)}, bf16[8,256,768]{2,1,0:T(8,128)(2,1)S(1)}, u32[]{:S(2)}, u32[]{:S(2)}) collective-permute-start(bf16[8,256,768]{2,1,0:T(8,128)(2,1)S(1)} %pad_maximum_fusion), channel_id=1, source_target_pairs={{0,8},{8,0},{1,9},{9,1},{2,10},{10,2},{3,11},{11,3},{4,12},{12,4},... | collective-permute-start | bytes 9437192 | tf_op jit(solution)/shard_map/ppermute | solution.py:100
  141.2 1.0 copy-start.10
  145.7 2.2 %copy-start.3 = (bf16[4096,512]{1,0:T(8,128)(2,1)S(1)}, bf16[4096,512]{1,0:T(8,128)(2,1)}, u32[]{:S(2)}) copy-start(bf16[4096,512]{1,0:T(8,128)(2,1)} %param.10) | copy-start | bytes 12582916
  148.0 1.4 copy-start.5
  150.1 6.0 %copy-start.13 = (bf16[256,1,64]{0,2,1:T(8,128)(2,1)S(1)}, bf16[256,1,64]{0,2,1:T(8,128)(2,1)}, u32[]{:S(2)}) copy-start(bf16[256,1,64]{0,2,1:T(8,128)(2,1)} %get-tuple-element.29) | copy-start | bytes 98308
  150.1 6.0 %copy-start.14 = (bf16[256,1,64]{0,2,1:T(8,128)(2,1)S(1)}, bf16[256,1,64]{0,2,1:T(8,128)(2,1)}, u32[]{:S(2)}) copy-start(bf16[256,1,64]{0,2,1:T(8,128)(2,1)} %get-tuple-element.30) | copy-start | bytes 98308
  151.6 29.3 %all-to-all-start.2 = ((bf16[8,512,256]{1,2,0:T(8,128)(2,1)}), bf16[8,512,256]{1,2,0:T(8,128)(2,1)}, u32[]{:S(2)}, u32[]{:S(2)}) async-start(bf16[8,512,256]{1,2,0:T(8,128)(2,1)} %bitcast.113), calls=%async_computation.2 | async-start | bytes 4194304 | tf_op jit(solution)/shard_map/all_to_all | solution.py:105
  156.9 2.7 %collective-permute-start.2 = (bf16[8,256,256]{2,1,0:T(8,128)(2,1)S(1)}, bf16[8,256,256]{2,1,0:T(8,128)(2,1)S(1)}, u32[]{:S(2)}, u32[]{:S(2)}) collective-permute-start(bf16[8,256,256]{2,1,0:T(8,128)(2,1)S(1)} %bitcast.125), channel_id=1, source_target_pairs={{0,8},{8,0},{1,9},{9,1},{2,10},{10,2},{3,11},{11,3},{4,12},{12,4},... | collective-permute-start | bytes 3145736 | tf_op jit(solution)/shard_map/ppermute | solution.py:100
  157.2 28.6 %copy-start.11 = (f32[256,768]{1,0:T(8,128)S(1)}, f32[256,768]{1,0:T(8,128)}, u32[]{:S(2)}) copy-start(f32[256,768]{1,0:T(8,128)} %copy-done.10) | copy-start | bytes 2359300
  180.9 20.6 %all-to-all-start.3 = ((bf16[8,256,256]{2,1,0:T(8,128)(2,1)}), bf16[8,256,256]{2,1,0:T(8,128)(2,1)S(1)}, u32[]{:S(2)}, u32[]{:S(2)}) async-start(bf16[8,256,256]{2,1,0:T(8,128)(2,1)} %add_convert_fusion), calls=%async_computation.3 | async-start | bytes 2097152 | tf_op jit(solution)/shard_map/all_to_all | solution.py:105

commit v2 on v0

--- a/solution.py
+++ b/solution.py
@@ -175,13 +175,9 @@
         odd = lax.dot_general(normed_odd, grads, tokens_first, preferred_element_type=jnp.float32)
         return jnp.where(first, even, odd), jnp.where(first, odd, even)
 
+    kv_total = scatter_sum(pair_sum(kv_terms[0], kv_terms[1]), ("seq_x", "seq_z"))
     wq_keep, wq_send = weight_halves(query_grad)
-    joint = pair_sum(
-        jnp.concatenate([kv_terms[0], wq_keep], axis=2), jnp.concatenate([kv_terms[1], wq_send], axis=2)
-    )
-    joint_total = scatter_sum(joint, ("seq_x", "seq_z"))
-    kv_total = joint_total[:, : 2 * HEAD]
-    grad_wq = joint_total[:, 2 * HEAD :]
+    grad_wq = scatter_sum(pair_sum(wq_keep, wq_send), ("seq_x", "seq_z"))
 
     def weight_terms(grads):
         keep, send = weight_halves(grads)

time: 196 us -> 190 us (0.969)
  blocking collectives: 44 us -> 0 us
  waiting for transfers between devices: 38.8 us -> 71 us
  starting transfers between devices: 17.6 us -> 27.5 us
  local copies, waits for them, and re-layouts: 24.4 us -> 22.2 us
    all_to_all x1 -> x0, blocking collectives: 44 us -> none  [scatter_sum(): arrived = lax.all_to_all(parts, axis, 0, 0, tiled=True)]
    all_to_all x2 -> x4, waiting for transfers between devices: 31.3 us -> 62.8 us  [scatter_sum(): arrived = lax.all_to_all(parts, axis, 0, 0, tiled=True)]
    all_to_all x2 -> x4, starting transfers between devices: 9.42 us -> 18.9 us  [scatter_sum(): arrived = lax.all_to_all(parts, axis, 0, 0, tiled=True)]
    select_n x2 -> x0, other arithmetic: 5.85 us -> none  [weight_halves(): return (jnp.where(first, even, odd), jnp.where(first, odd, even))]
    convert_element_type x2 -> x3, other arithmetic: 4.34 us -> 9.56 us  [pair_sum(): (keep.astype(jnp.float32) + got.astype(jnp.float32)).astype(jnp.bfloat16)]
    reduce_sum x3 -> x4, other arithmetic: 3.25 us -> 6.52 us  [scatter_sum(): return jnp.sum(arrived.astype(jnp.float32), axis=0)]
    convert_element_type x2 -> x1, local copies, waits for them, and re-layouts: 5.16 us -> 2.04 us  [pair_sum(): keep.astype(jnp.float32) + got.astype(jnp.float32)]
    dot_general x6, matrix products: 19.9 us -> 22.7 us  [product(): return jnp.einsum(form, left, right, preferred_element_type=jnp.float32)]
  transfers between devices with their start and end apart: 6 -> 9, of which waited for: 5 -> 7; matrix products, arithmetic and copies ran while one was open for 14% -> 24% of each run, Pallas kernels for 0% -> 0%
where the time goes in v2:
time: 190 us; the launch traced here: 189 us
  waiting for transfers between devices  71 us (37%)
  matrix products  35.5 us (19%)
  other arithmetic  32 us (17%)
  starting transfers between devices  27.5 us (14%)
  local copies, waits for them, and re-layouts  22.2 us (12%)
    all_to_all x4, waiting for transfers between devices, scatter_sum(): arrived = lax.all_to_all(parts, axis, 0, 0, tiled=True)  62.8 us
    dot_general x6, matrix products, product(): return jnp.einsum(form, left, right, preferred_element_type=jnp.float32)  22.7 us
    all_to_all x4, starting transfers between devices, scatter_sum(): arrived = lax.all_to_all(parts, axis, 0, 0, tiled=True)  18.9 us
    unnamed x41, local copies, waits for them, and re-layouts  9.98 us
    convert_element_type x3, other arithmetic, pair_sum(): (keep.astype(jnp.float32) + got.astype(jnp.float32)).astype(jnp.bfloat16)  9.56 us
    all_to_all x1, starting transfers between devices, gather_rows(): mine = lax.all_to_all(copies, ('seq_x', 'seq_z'), 0, 0, tiled=True)  7.99 us
    reduce_sum x4, other arithmetic, scatter_sum(): return jnp.sum(arrived.astype(jnp.float32), axis=0)  6.52 us
    all_to_all x1, waiting for transfers between devices, gather_rows(): mine = lax.all_to_all(copies, ('seq_x', 'seq_z'), 0, 0, tiled=True)  4.65 us
  transfers between devices with their start and end apart: 9, of which 7 were waited for; matrix products, arithmetic and copies ran while one was open for 24% of the time, Pallas kernels for 0%

profile of v2, /device:TPU:0, one launch (start us, length us, event | category | flops | bytes accessed | tf_op | source)
XLA Modules:
  0.0 189.4 jit_solution(9433695560567495777)
XLA Ops:
  1.9 2.4 %convolution_bitcast_fusion.3 = f32[256,1,128]{0,2,1:T(8,128)S(1)} fusion(bf16[256,4096]{1,0:T(8,128)(2,1)} %param.9, bf16[4096,128]{1,0:T(8,128)(2,1)S(1)} %copy-done), kind=kOutput, calls=%fused_computation.50 | convolution fusion | flops 268435456 | bytes 3276800 | tf_op jit(solution)/shard_map/dot_general | solution.py:122
  4.4 0.8 convolution_convert_fusion
  5.7 1.0 broadcast_in_dim.111
  6.7 8.0 %all-to-all-start = ((bf16[8,256,256]{2,1,0:T(8,128)(2,1)}), bf16[8,256,256]{2,1,0:T(8,128)(2,1)}, u32[]{:S(2)}, u32[]{:S(2)}) async-start(bf16[8,256,256]{2,1,0:T(8,128)(2,1)} %broadcast_in_dim.111), calls=%async_computation | async-start | bytes 2097152 | tf_op jit(solution)/shard_map/all_to_all | solution.py:93
  14.8 2.5 %copy.87 = bf16[256,4096]{0,1:T(8,128)(2,1)} copy(bf16[256,4096]{1,0:T(8,128)(2,1)S(1)} %copy-done.4) | data formatting | bytes 4194304 | tf_op args[0]
  18.4 4.3 %fusion.69 = f32[256,512]{1,0:T(8,128)} fusion(bf16[256,4096]{1,0:T(8,128)(2,1)S(1)} %copy-done.4, bf16[4096,512]{1,0:T(8,128)(2,1)} %param.10), kind=kOutput, calls=%fused_computation.163 | convolution fusion | flops 1073741824 | bytes 6815744 | tf_op jit(solution)/shard_map/dot_general | solution.py:119
  22.7 1.2 reshape.435
  24.1 1.8 bitcast_and_fusion
  26.0 4.7 %all-to-all-done = bf16[8,256,256]{2,1,0:T(8,128)(2,1)} async-done(((bf16[8,256,256]{2,1,0:T(8,128)(2,1)}), bf16[8,256,256]{2,1,0:T(8,128)(2,1)}, u32[]{:S(2)}, u32[]{:S(2)}) %all-to-all-start) | async-done | bytes 1048608 | tf_op jit(solution)/shard_map/all_to_all | solution.py:93
  31.8 0.9 dynamic-slice_bitcast_fusion
  32.7 0.8 collective-permute-done
  33.5 2.0 %fusion.15 = bf16[2,3,2,256,256]{4,3,2,1,0:T(8,128)(2,1)S(1)} fusion(s32[]{:T(128)S(6)} %select_n.303, bf16[1,4,2,256,256]{4,3,2,1,0:T(8,128)(2,1)} %bitcast.4, bf16[1,4,2,256,256]{4,3,2,1,0:T(8,128)(2,1)S(1)} %bitcast.144), kind=kLoop, calls=%fused_computation.45 | loop fusion | flops 2359296 | bytes 3670020 | tf_op jit(solution)/shard_map/jit(_roll_dynamic)/concatenate | solution.py:133
  35.7 2.4 %fusion.67 = (f32[4,256]{1,0:T(4,128)S(1)}, f32[4,256,3328]{1,2,0:T(8,128)S(1)}) fusion(bf16[256,4,64]{2,0,1:T(8,128)(2,1)S(1)} %get-tuple-element.18, bf16[256,4,64]{2,0,1:T(8,128)(2,1)S(1)} %get-tuple-element.17, bf16[3328,256]{1,0:T(8,128)(2,1)S(1)} %bitcast.140, pred[256,3328]{0,1:T(8,128)(4,1)S(1)} %copy-done.12), kind=kOutput, calls=%fused_computation.161 | convolution fusion | flops 883162112 | bytes 15863808 | tf_op jit(solution)/shard_map/tgd,sd->gts/dot_general | solution.py:45
  38.1 1.8 exponential_reduce_fusion
  40.0 4.2 %fusion.6 = bf16[3328,128]{0,1:T(8,128)(2,1)S(1)} fusion(bf16[256,4,128]{0,2,1:T(8,128)(2,1)S(1)} %bitcast.146, f32[4,256,3328]{1,2,0:T(8,128)S(1)} %get-tuple-element.33, f32[4,256]{1,0:T(4,128)S(1)} %log_add_fusion, pred[256,3328]{0,1:T(8,128)(4,1)} %bitcast_and_fusion), kind=kOutput, calls=%fused_computation.15 | convolution fusion | flops 883064832 | bytes 15601664 | tf_op jit(solution)/shard_map/gts,tgd->sd/dot_general | solution.py:45
  44.2 2.4 %fusion.17 = f32[4,256]{1,0:T(4,128)S(1)} fusion(bf16[3328,256]{1,0:T(8,128)(2,1)S(1)} %bitcast.142, f32[4,256,3328]{1,2,0:T(8,128)S(1)} %get-tuple-element.33, f32[4,256]{1,0:T(4,128)S(1)} %log_add_fusion, pred[256,3328]{0,1:T(8,128)(4,1)S(1)} %copy-done.13, bf16[256,4,128]{0,2,1:T(8,128)(2,1)S(1)} %bitcast.147), kind=kOutput, calls=%fused_computation.49 | convolution fusion | flops 883031040 | bytes 15605760 | tf_op jit(solution)/shard_map/gts,sd->gtd/dot_general | solution.py:45
  46.6 5.4 %fusion.2 = bf16[4,256,3328]{1,2,0:T(8,128)(2,1)S(1)} fusion(f32[4,256,3328]{1,2,0:T(8,128)S(1)} %get-tuple-element.33, bf16[256,4,128]{0,2,1:T(8,128)(2,1)S(1)} %bitcast.148, f32[4,256]{1,0:T(4,128)S(1)} %fusion.17, f32[4,256]{1,0:T(4,128)S(1)} %log_add_fusion, pred[256,3328]{0,1:T(8,128)(4,1)} %bitcast_and_fusion, bf16[3328,256]{1,0:T(8,128)(2,1)S(1)} %bitcast.143), kind=kOutput, calls=%fused_computation.4 | convolution fusion | flops 892862464 | bytes 22421504 | tf_op jit(solution)/shard_map/tgd,sd->gts/dot_general | solution.py:45
  52.0 2.4 %fusion.5 = bf16[3328,128]{0,1:T(8,128)(2,1)S(1)} fusion(bf16[4,256,3328]{1,2,0:T(8,128)(2,1)S(1)} %fusion.2, bf16[256,4,64]{2,0,1:T(8,128)(2,1)S(1)} %get-tuple-element.18, bf16[256,4,64]{2,0,1:T(8,128)(2,1)S(1)} %get-tuple-element.17), kind=kOutput, calls=%fused_computation.14 | convolution fusion | flops 873365504 | bytes 7929856 | tf_op jit(solution)/shard_map/gts,tgd->sd/dot_general | solution.py:45
  54.8 1.4 fusion.13
  56.3 1.7 copy.82
  58.1 1.4 fusion.10
  59.5 1.1 fusion.64
  60.6 1.3 copy.84
  62.1 1.4 bitcast_convert_fusion
  63.5 2.0 %copy.85 = f32[8,256,256]{1,2,0:T(8,128)} copy(f32[8,256,256]{2,1,0:T(8,128)S(1)} %bitcast_convert_fusion) | data formatting | bytes 4194304 | tf_op jit(solution)/shard_map/convert_element_type | solution.py:101
  65.5 6.0 %convolution_bitcast_fusion.2 = f32[256,4,128]{2,0,1:T(8,128)S(1)} fusion(bf16[4,256,3328]{1,2,0:T(8,128)(2,1)} %copy-done.1, bf16[3328,256]{1,0:T(8,128)(2,1)} %bitcast.141), kind=kOutput, calls=%fused_computation.48 | convolution fusion | flops 872415232 | bytes 8192000 | tf_op jit(solution)/shard_map/gts,sd->tgd/dot_general | solution.py:45
  72.1 3.2 %add_convert_fusion = bf16[8,256,256]{1,2,0:T(8,128)(2,1)} fusion(f32[8,256,256]{1,2,0:T(8,128)} %copy.85, bf16[8,256,256]{1,2,0:T(8,128)(2,1)} %collective-permute-done.1), kind=kLoop, calls=%fused_computation.39 | loop fusion | flops 1572864 | bytes 4194304 | tf_op jit(solution)/shard_map/convert_element_type | solution.py:101
  75.3 4.2 %all-to-all-start.1 = ((bf16[8,256,256]{1,2,0:T(8,128)(2,1)}), bf16[8,256,256]{1,2,0:T(8,128)(2,1)}, u32[]{:S(2)}, u32[]{:S(2)}) async-start(bf16[8,256,256]{1,2,0:T(8,128)(2,1)} %add_convert_fusion), calls=%async_computation.1 | async-start | bytes 2097152 | tf_op jit(solution)/shard_map/all_to_all | solution.py:105
  81.1 2.4 %fusion.8 = bf16[8,256,512]{1,2,0:T(8,128)(2,1)} fusion(f32[512,8,256]{2,0,1:T(8,128)S(1)} %fusion.22, f32[512,8,256]{2,0,1:T(8,128)S(1)} %fusion.20, pred[]{:T(512)S(6)} %eq.63), kind=kLoop, calls=%fused_computation.29 | loop fusion | flops 1048576 | bytes 10485761 | tf_op jit(solution)/shard_map/convert_element_type | solution.py:100
  84.6 11.0 %all-to-all-done.1 = bf16[8,256,256]{1,2,0:T(8,128)(2,1)} async-done(((bf16[8,256,256]{1,2,0:T(8,128)(2,1)}), bf16[8,256,256]{1,2,0:T(8,128)(2,1)}, u32[]{:S(2)}, u32[]{:S(2)}) %all-to-all-start.1) | async-done | bytes 1048608 | tf_op jit(solution)/shard_map/all_to_all | solution.py:105
  95.5 1.4 convert_reduce_fusion.2
  98.1 1.1 copy-done.6
  99.1 1.3 convolution_add_fusion
  101.2 1.5 copy.115
  102.7 4.8 %all-to-all-start.2 = ((bf16[8,512,256]{1,2,0:T(8,128)(2,1)}), bf16[8,512,256]{1,2,0:T(8,128)(2,1)}, u32[]{:S(2)}, u32[]{:S(2)}) async-start(bf16[8,512,256]{1,2,0:T(8,128)(2,1)} %bitcast.133), calls=%async_computation.2 | async-start | bytes 4194304 | tf_op jit(solution)/shard_map/all_to_all | solution.py:105
  109.0 2.6 %collective-permute-done.3 = bf16[8,256,256]{1,2,0:T(8,128)(2,1)S(1)} collective-permute-done((bf16[8,256,256]{1,2,0:T(8,128)(2,1)S(1)}, bf16[8,256,256]{1,2,0:T(8,128)(2,1)S(1)}, u32[]{:S(2)}, u32[]{:S(2)}) %collective-permute-start.3) | collective-permute-done | bytes 1048608 | tf_op jit(solution)/shard_map/ppermute | solution.py:100
  111.6 1.4 fusion.12
  113.1 20.1 %all-to-all-done.2 = bf16[8,512,256]{1,2,0:T(8,128)(2,1)} async-done(((bf16[8,512,256]{1,2,0:T(8,128)(2,1)}), bf16[8,512,256]{1,2,0:T(8,128)(2,1)}, u32[]{:S(2)}, u32[]{:S(2)}) %all-to-all-start.2) | async-done | bytes 2097184 | tf_op jit(solution)/shard_map/all_to_all | solution.py:105
  133.1 5.8 %all-to-all-start.4 = ((bf16[8,256,256]{1,2,0:T(8,128)(2,1)}), bf16[8,256,256]{1,2,0:T(8,128)(2,1)S(1)}, u32[]{:S(2)}, u32[]{:S(2)}) async-start(bf16[8,256,256]{1,2,0:T(8,128)(2,1)} %fusion.12), calls=%async_computation.4 | async-start | bytes 2097152 | tf_op jit(solution)/shard_map/all_to_all | solution.py:105
  138.9 4.9 %fusion.7 = bf16[8,256,512]{1,2,0:T(8,128)(2,1)} fusion(bf16[8,256,512]{1,2,0:T(8,128)(2,1)} %collective-permute-done.2, f32[512,8,256]{2,0,1:T(8,128)} %copy-done.2, f32[512,8,256]{2,0,1:T(8,128)} %copy-done.3, pred[]{:T(512)S(6)} %eq.63), kind=kLoop, calls=%fused_computation.25 | loop fusion | flops 4194304 | bytes 12582913 | tf_op jit(solution)/shard_map/convert_element_type | solution.py:101
  143.9 10.8 %all-to-all-done.4 = bf16[8,256,256]{1,2,0:T(8,128)(2,1)S(1)} async-done(((bf16[8,256,256]{1,2,0:T(8,128)(2,1)}), bf16[8,256,256]{1,2,0:T(8,128)(2,1)S(1)}, u32[]{:S(2)}, u32[]{:S(2)}) %all-to-all-start.4) | async-done | bytes 1048608 | tf_op jit(solution)/shard_map/all_to_all | solution.py:105
  154.6 1.0 copy-done.9
  155.6 4.1 %all-to-all-start.3 = ((bf16[8,256,512]{1,2,0:T(8,128)(2,1)}), bf16[8,256,512]{1,2,0:T(8,128)(2,1)S(1)}, u32[]{:S(2)}, u32[]{:S(2)}) async-start(bf16[8,256,512]{1,2,0:T(8,128)(2,1)} %fusion.7), calls=%async_computation.3 | async-start | bytes 4194304 | tf_op jit(solution)/shard_map/all_to_all | solution.py:105
  159.7 2.7 %reduce_sum.60 = bf16[512,256]{0,1:T(8,128)(2,1)} reduce(bf16[8,512,256]{1,2,0:T(8,128)(2,1)} %all-to-all-done.2, bf16[]{:T(256)} %constant.216.clone.1), dimensions={0}, to_apply=%region_4.6 | reduce | flops 917504 | bytes 2359298 | tf_op jit(solution)/shard_map/reduce_sum | solution.py:106
  162.4 1.4 convert_reduce_fusion.1
  165.3 21.0 %all-to-all-done.3 = bf16[8,256,512]{1,2,0:T(8,128)(2,1)S(1)} async-done(((bf16[8,256,512]{1,2,0:T(8,128)(2,1)}), bf16[8,256,512]{1,2,0:T(8,128)(2,1)S(1)}, u32[]{:S(2)}, u32[]{:S(2)}) %all-to-all-start.3) | async-done | bytes 2097184 | tf_op jit(solution)/shard_map/all_to_all | solution.py:105
  186.3 1.1 convert_reduce_fusion
  187.4 2.0 %copy.90 = f32[256,512]{1,0:T(8,128)} copy(f32[256,512]{0,1:T(8,128)} %convert_reduce_fusion) | data formatting | bytes 1048576
  (86 shorter events, 12.9 us)
Async XLA Ops:
  0.6 1.2 copy-start
  0.6 3.7 %copy-start.4 = (bf16[256,4096]{1,0:T(8,128)(2,1)S(1)}, bf16[256,4096]{1,0:T(8,128)(2,1)}, u32[]{:S(2)}) copy-start(bf16[256,4096]{1,0:T(8,128)(2,1)} %param.9) | copy-start | bytes 6291460
  0.7 3.7 %copy-start.7 = (bf16[4096,128]{1,0:T(8,128)(2,1)S(1)}, bf16[4096,128]{1,0:T(8,128)(2,1)}, u32[]{:S(2)}) copy-start(bf16[4096,128]{1,0:T(8,128)(2,1)} %param.12) | copy-start | bytes 3145732
  6.7 10.7 %copy-start.15 = (s32[2,32]{1,0:T(2,128)S(1)}, s32[2,32]{1,0:T(2,128)}, u32[]{:S(2)}) copy-start(s32[2,32]{1,0:T(2,128)} %param.14) | copy-start | bytes 772
  6.7 23.9 %all-to-all-start = ((bf16[8,256,256]{2,1,0:T(8,128)(2,1)}), bf16[8,256,256]{2,1,0:T(8,128)(2,1)}, u32[]{:S(2)}, u32[]{:S(2)}) async-start(bf16[8,256,256]{2,1,0:T(8,128)(2,1)} %broadcast_in_dim.111), calls=%async_computation | async-start | bytes 2097152 | tf_op jit(solution)/shard_map/all_to_all | solution.py:93
  18.4 5.5 %copy-start.14 = (bf16[256,512]{1,0:T(8,128)(2,1)S(1)}, bf16[256,512]{1,0:T(8,128)(2,1)}, u32[]{:S(2)}) copy-start(bf16[256,512]{1,0:T(8,128)(2,1)} %param.15) | copy-start | bytes 786436
  30.7 2.9 %collective-permute-start = (bf16[8,256,256]{2,1,0:T(8,128)(2,1)}, bf16[8,256,256]{2,1,0:T(8,128)(2,1)S(1)}, u32[]{:S(2)}, u32[]{:S(2)}) collective-permute-start(bf16[8,256,256]{2,1,0:T(8,128)(2,1)} %all-to-all-done), channel_id=1, source_target_pairs={{0,8},{8,0},{1,9},{9,1},{2,10},{10,2},{3,11},{11,3},{4,12},{12,4},... | collective-permute-start | bytes 3145736 | tf_op jit(solution)/shard_map/ppermute | solution.py:94
  33.5 2.2 %copy-start.12 = (pred[256,3328]{0,1:T(8,128)(4,1)S(1)}, pred[256,3328]{0,1:T(8,128)(4,1)}, u32[]{:S(2)}) copy-start(pred[256,3328]{0,1:T(8,128)(4,1)} %bitcast_and_fusion) | copy-start | bytes 2555908
  35.7 2.5 %copy-start.10 = (bf16[13,256,256]{2,1,0:T(8,128)(2,1)}, bf16[13,256,256]{2,1,0:T(8,128)(2,1)S(1)}, u32[]{:S(2)}) copy-start(bf16[13,256,256]{2,1,0:T(8,128)(2,1)S(1)} %pad_maximum_fusion) | copy-start | bytes 5111812
  40.0 4.2 %copy-start.11 = (bf16[13,256,256]{2,1,0:T(8,128)(2,1)S(1)}, bf16[13,256,256]{2,1,0:T(8,128)(2,1)}, u32[]{:S(2)}) copy-start(bf16[13,256,256]{2,1,0:T(8,128)(2,1)} %copy-done.10) | copy-start | bytes 5111812
  40.0 4.2 %copy-start.13 = (pred[256,3328]{0,1:T(8,128)(4,1)S(1)}, pred[256,3328]{0,1:T(8,128)(4,1)}, u32[]{:S(2)}) copy-start(pred[256,3328]{0,1:T(8,128)(4,1)} %bitcast_and_fusion) | copy-start | bytes 2555908
  51.9 2.8 %copy-start.1 = (bf16[4,256,3328]{1,2,0:T(8,128)(2,1)}, bf16[4,256,3328]{1,2,0:T(8,128)(2,1)S(1)}, u32[]{:S(2)}) copy-start(bf16[4,256,3328]{1,2,0:T(8,128)(2,1)S(1)} %fusion.2) | copy-start | bytes 20447236
  61.9 10.1 %collective-permute-start.1 = (bf16[8,256,256]{1,2,0:T(8,128)(2,1)}, bf16[8,256,256]{1,2,0:T(8,128)(2,1)}, u32[]{:S(2)}, u32[]{:S(2)}) collective-permute-start(bf16[8,256,256]{1,2,0:T(8,128)(2,1)} %copy.84), channel_id=1, source_target_pairs={{0,8},{8,0},{1,9},{9,1},{2,10},{10,2},{3,11},{11,3},{4,12},{12,4},... | collective-permute-start | bytes 3145736 | tf_op jit(solution)/shard_map/ppermute | solution.py:100
  72.1 7.5 %copy-start.5 = (bf16[256,4096]{0,1:T(8,128)(2,1)S(1)}, bf16[256,4096]{0,1:T(8,128)(2,1)}, u32[]{:S(2)}) copy-start(bf16[256,4096]{0,1:T(8,128)(2,1)} %copy.87) | copy-start | bytes 6291460
  75.3 20.2 %all-to-all-start.1 = ((bf16[8,256,256]{1,2,0:T(8,128)(2,1)}), bf16[8,256,256]{1,2,0:T(8,128)(2,1)}, u32[]{:S(2)}, u32[]{:S(2)}) async-start(bf16[8,256,256]{1,2,0:T(8,128)(2,1)} %add_convert_fusion), calls=%async_computation.1 | async-start | bytes 2097152 | tf_op jit(solution)/shard_map/all_to_all | solution.py:105
  80.3 3.2 %copy-start.2 = (f32[512,8,256]{2,0,1:T(8,128)}, f32[512,8,256]{2,0,1:T(8,128)S(1)}, u32[]{:S(2)}) copy-start(f32[512,8,256]{2,0,1:T(8,128)S(1)} %fusion.20) | copy-start | bytes 12582916
  81.1 3.1 %copy-start.3 = (f32[512,8,256]{2,0,1:T(8,128)}, f32[512,8,256]{2,0,1:T(8,128)S(1)}, u32[]{:S(2)}) copy-start(f32[512,8,256]{2,0,1:T(8,128)S(1)} %fusion.22) | copy-start | bytes 12582916
  84.2 54.7 %collective-permute-start.2 = (bf16[8,256,512]{1,2,0:T(8,128)(2,1)}, bf16[8,256,512]{1,2,0:T(8,128)(2,1)}, u32[]{:S(2)}, u32[]{:S(2)}) collective-permute-start(bf16[8,256,512]{1,2,0:T(8,128)(2,1)} %fusion.8), channel_id=1, source_target_pairs={{0,8},{8,0},{1,9},{9,1},{2,10},{10,2},{3,11},{11,3},{4,12},{12,4},... | collective-permute-start | bytes 6291464 | tf_op jit(solution)/shard_map/ppermute | solution.py:100
  96.9 2.2 %copy-start.6 = (bf16[4096,512]{1,0:T(8,128)(2,1)S(1)}, bf16[4096,512]{1,0:T(8,128)(2,1)}, u32[]{:S(2)}) copy-start(bf16[4096,512]{1,0:T(8,128)(2,1)} %param.10) | copy-start | bytes 12582916
  99.1 1.4 copy-start.8
  102.7 30.4 %all-to-all-start.2 = ((bf16[8,512,256]{1,2,0:T(8,128)(2,1)}), bf16[8,512,256]{1,2,0:T(8,128)(2,1)}, u32[]{:S(2)}, u32[]{:S(2)}) async-start(bf16[8,512,256]{1,2,0:T(8,128)(2,1)} %bitcast.133), calls=%async_computation.2 | async-start | bytes 4194304 | tf_op jit(solution)/shard_map/all_to_all | solution.py:105
  108.9 2.7 %collective-permute-start.3 = (bf16[8,256,256]{1,2,0:T(8,128)(2,1)S(1)}, bf16[8,256,256]{1,2,0:T(8,128)(2,1)S(1)}, u32[]{:S(2)}, u32[]{:S(2)}) collective-permute-start(bf16[8,256,256]{1,2,0:T(8,128)(2,1)S(1)} %fusion.18), channel_id=1, source_target_pairs={{0,8},{8,0},{1,9},{9,1},{2,10},{10,2},{3,11},{11,3},{4,12},{12,4},... | collective-permute-start | bytes 3145736 | tf_op jit(solution)/shard_map/ppermute | solution.py:100
  133.1 21.5 %all-to-all-start.4 = ((bf16[8,256,256]{1,2,0:T(8,128)(2,1)}), bf16[8,256,256]{1,2,0:T(8,128)(2,1)S(1)}, u32[]{:S(2)}, u32[]{:S(2)}) async-start(bf16[8,256,256]{1,2,0:T(8,128)(2,1)} %fusion.12), calls=%async_computation.4 | async-start | bytes 2097152 | tf_op jit(solution)/shard_map/all_to_all | solution.py:105
  154.6 1.0 copy-start.9
  155.6 30.7 %all-to-all-start.3 = ((bf16[8,256,512]{1,2,0:T(8,128)(2,1)}), bf16[8,256,512]{1,2,0:T(8,128)(2,1)S(1)}, u32[]{:S(2)}, u32[]{:S(2)}) async-start(bf16[8,256,512]{1,2,0:T(8,128)(2,1)} %fusion.7), calls=%async_computation.3 | async-start | bytes 4194304 | tf_op jit(solution)/shard_map/all_to_all | solution.py:105

commit v3 on v2

--- a/solution.py
+++ b/solution.py
@@ -177,7 +177,6 @@
 
     kv_total = scatter_sum(pair_sum(kv_terms[0], kv_terms[1]), ("seq_x", "seq_z"))
     wq_keep, wq_send = weight_halves(query_grad)
-    grad_wq = scatter_sum(pair_sum(wq_keep, wq_send), ("seq_x", "seq_z"))
 
     def weight_terms(grads):
         keep, send = weight_halves(grads)
@@ -190,9 +189,15 @@
     key_grad = rotate(kv_total[:, :HEAD], positions, -1.0).astype(jnp.bfloat16)
     value_grad = kv_total[:, HEAD:].astype(jnp.bfloat16)
     kv_grad = jnp.concatenate([key_grad, value_grad], axis=1)
-    grad_wkv = weight_terms(kv_grad)
-    grad_wk = grad_wkv[:, :HEAD]
-    grad_wv = grad_wkv[:, HEAD:]
+    wkv_keep, wkv_send = weight_halves(kv_grad)
+    grad_w = scatter_sum(
+        pair_sum(jnp.concatenate([wq_keep, wkv_keep], axis=-1), jnp.concatenate([wq_send, wkv_send], axis=-1)),
+        ("seq_x", "seq_z"),
+    )
+    query_cols = wq_keep.shape[-1]
+    grad_wq = grad_w[:, :query_cols]
+    grad_wk = grad_w[:, query_cols : query_cols + HEAD]
+    grad_wv = grad_w[:, query_cols + HEAD :]
     partial_input = partial_input + lax.dot_general(
         w_key, key_grad, contract, preferred_element_type=jnp.float32
     )

time: 190 us -> 192 us (1.011)
  starting transfers between devices: 27.5 us -> 23.1 us
  local copies, waits for them, and re-layouts: 22.2 us -> 26.1 us
  other arithmetic: 32 us -> 35.6 us
  waiting for transfers between devices: 71 us -> 67.4 us
  matrix products: 35.5 us -> 37.5 us
    select_n x0 -> x4, other arithmetic: none -> 5.56 us  [weight_halves(): return (jnp.where(first, even, odd), jnp.where(first, odd, even))]
    all_to_all x4 -> x3, starting transfers between devices: 18.9 us -> 15.1 us  [scatter_sum(): arrived = lax.all_to_all(parts, axis, 0, 0, tiled=True)]
    unnamed x41 -> x45, local copies, waits for them, and re-layouts: 9.98 us -> 12.9 us
    convert_element_type x2 -> x0, other arithmetic: 2.83 us -> none  [pair_sum(): got = lax.ppermute(send.astype(jnp.bfloat16), 'seq_core', PAIR)]
    ppermute x3 -> x2, waiting for transfers between devices: 2.65 us -> 0.01 us  [pair_sum(): got = lax.ppermute(send.astype(jnp.bfloat16), 'seq_core', PAIR)]
    concatenate x0 -> x1, other arithmetic: none -> 1.94 us  [body(): jnp.concatenate([wq_send, wkv_send], axis=-1)]
    dot_general x1, matrix products: 0.85 us -> 2.77 us  [body(): jnp.dot(normed, w_value, preferred_element_type=jnp.float32)]
    convert_element_type x3 -> x2, other arithmetic: 9.56 us -> 7.65 us  [pair_sum(): (keep.astype(jnp.float32) + got.astype(jnp.float32)).astype(jnp.bfloat16)]
  transfers between devices with their start and end apart: 9 -> 7, of which waited for: 7 -> 5; matrix products, arithmetic and copies ran while one was open for 24% -> 22% of each run, Pallas kernels for 0% -> 0%
where the time goes in v3:
time: 192 us; the launch traced here: 191 us
  waiting for transfers between devices  67.4 us (35%)
  matrix products  37.5 us (20%)
  other arithmetic  35.6 us (19%)
  local copies, waits for them, and re-layouts  26.1 us (14%)
  starting transfers between devices  23.1 us (12%)
    all_to_all x3, waiting for transfers between devices, scatter_sum(): arrived = lax.all_to_all(parts, axis, 0, 0, tiled=True)  62 us
    dot_general x6, matrix products, product(): return jnp.einsum(form, left, right, preferred_element_type=jnp.float32)  23.2 us
    all_to_all x3, starting transfers between devices, scatter_sum(): arrived = lax.all_to_all(parts, axis, 0, 0, tiled=True)  15.1 us
    unnamed x45, local copies, waits for them, and re-layouts  12.9 us
    all_to_all x1, starting transfers between devices, gather_rows(): mine = lax.all_to_all(copies, ('seq_x', 'seq_z'), 0, 0, tiled=True)  7.86 us
    convert_element_type x2, other arithmetic, pair_sum(): (keep.astype(jnp.float32) + got.astype(jnp.float32)).astype(jnp.bfloat16)  7.65 us
    reduce_sum x3, other arithmetic, scatter_sum(): return jnp.sum(arrived.astype(jnp.float32), axis=0)  6.6 us
    select_n x4, other arithmetic, weight_halves(): return (jnp.where(first, even, odd), jnp.where(first, odd, even))  5.56 us
  transfers between devices with their start and end apart: 7, of which 5 were waited for; matrix products, arithmetic and copies ran while one was open for 22% of the time, Pallas kernels for 0%

profile of v3, /device:TPU:0, one launch (start us, length us, event | category | flops | bytes accessed | tf_op | source)
XLA Modules:
  0.0 190.8 jit_solution(6925094877348682983)
XLA Ops:
  1.5 2.8 %convolution_convert_fusion = bf16[256,128]{0,1:T(8,128)(2,1)S(1)} fusion(bf16[256,4096]{1,0:T(8,128)(2,1)} %param.9, bf16[4096,128]{1,0:T(8,128)(2,1)} %param.12), kind=kOutput, calls=%fused_computation.51 | convolution fusion | flops 268468224 | bytes 3211264 | tf_op jit(solution)/shard_map/dot_general | solution.py:124
  5.6 1.0 broadcast_in_dim.111
  6.6 7.9 %all-to-all-start = ((bf16[8,256,256]{2,1,0:T(8,128)(2,1)}), bf16[8,256,256]{2,1,0:T(8,128)(2,1)}, u32[]{:S(2)}, u32[]{:S(2)}) async-start(bf16[8,256,256]{2,1,0:T(8,128)(2,1)} %broadcast_in_dim.111), calls=%async_computation | async-start | bytes 2097152 | tf_op jit(solution)/shard_map/all_to_all | solution.py:93
  14.6 2.6 %copy.87 = bf16[256,4096]{0,1:T(8,128)(2,1)} copy(bf16[256,4096]{1,0:T(8,128)(2,1)S(1)} %copy-done.6) | data formatting | bytes 4194304 | tf_op args[0]
  17.2 4.3 %fusion.68 = f32[256,512]{1,0:T(8,128)} fusion(bf16[256,4096]{1,0:T(8,128)(2,1)S(1)} %copy-done.6, bf16[4096,512]{1,0:T(8,128)(2,1)} %param.10), kind=kOutput, calls=%fused_computation.163 | convolution fusion | flops 1073741824 | bytes 6815744 | tf_op jit(solution)/shard_map/dot_general | solution.py:119
  21.4 1.2 reshape.435
  24.0 1.9 bitcast_and_fusion
  25.9 4.6 %all-to-all-done = bf16[8,256,256]{2,1,0:T(8,128)(2,1)} async-done(((bf16[8,256,256]{2,1,0:T(8,128)(2,1)}), bf16[8,256,256]{2,1,0:T(8,128)(2,1)}, u32[]{:S(2)}, u32[]{:S(2)}) %all-to-all-start) | async-done | bytes 1048608 | tf_op jit(solution)/shard_map/all_to_all | solution.py:93
  31.6 0.9 dynamic-slice_bitcast_fusion
  33.3 2.0 %fusion.14 = bf16[2,3,2,256,256]{4,3,2,1,0:T(8,128)(2,1)S(1)} fusion(s32[]{:T(128)S(6)} %select_n.309, bf16[1,4,2,256,256]{4,3,2,1,0:T(8,128)(2,1)} %bitcast.4, bf16[1,4,2,256,256]{4,3,2,1,0:T(8,128)(2,1)S(1)} %bitcast.140), kind=kLoop, calls=%fused_computation.45 | loop fusion | flops 2359296 | bytes 3670020 | tf_op jit(solution)/shard_map/jit(_roll_dynamic)/concatenate | solution.py:133
  35.5 2.4 %fusion.66 = (f32[4,256]{1,0:T(4,128)S(1)}, f32[4,256,3328]{1,2,0:T(8,128)S(1)}) fusion(bf16[256,4,64]{2,0,1:T(8,128)(2,1)S(1)} %get-tuple-element.18, bf16[256,4,64]{2,0,1:T(8,128)(2,1)S(1)} %get-tuple-element.17, bf16[3328,256]{1,0:T(8,128)(2,1)S(1)} %bitcast.136, pred[256,3328]{0,1:T(8,128)(4,1)S(1)} %copy-done.14), kind=kOutput, calls=%fused_computation.161 | convolution fusion | flops 883162112 | bytes 15863808 | tf_op jit(solution)/shard_map/tgd,sd->gts/dot_general | solution.py:45
  37.9 1.8 exponential_reduce_fusion
  39.8 3.9 %fusion.16 = f32[4,256]{1,0:T(4,128)S(1)} fusion(bf16[3328,256]{1,0:T(8,128)(2,1)} %bitcast.137, f32[4,256,3328]{1,2,0:T(8,128)S(1)} %get-tuple-element.33, f32[4,256]{1,0:T(4,128)S(1)} %log_add_fusion, pred[256,3328]{0,1:T(8,128)(4,1)} %bitcast_and_fusion, bf16[256,4,128]{0,2,1:T(8,128)(2,1)S(1)} %bitcast.142), kind=kOutput, calls=%fused_computation.49 | convolution fusion | flops 883031040 | bytes 15605760 | tf_op jit(solution)/shard_map/gts,sd->gtd/dot_general | solution.py:45
  43.6 3.1 %fusion.7 = bf16[3328,128]{0,1:T(8,128)(2,1)S(1)} fusion(bf16[256,4,128]{0,2,1:T(8,128)(2,1)S(1)} %bitcast.143, f32[4,256,3328]{1,2,0:T(8,128)S(1)} %get-tuple-element.33, f32[4,256]{1,0:T(4,128)S(1)} %log_add_fusion, pred[256,3328]{0,1:T(8,128)(4,1)S(1)} %copy-done.15), kind=kOutput, calls=%fused_computation.18 | convolution fusion | flops 883064832 | bytes 15601664 | tf_op jit(solution)/shard_map/gts,tgd->sd/dot_general | solution.py:45
  46.7 5.4 %fusion.2 = bf16[4,256,3328]{1,2,0:T(8,128)(2,1)S(1)} fusion(f32[4,256,3328]{1,2,0:T(8,128)S(1)} %get-tuple-element.33, bf16[256,4,128]{0,2,1:T(8,128)(2,1)S(1)} %bitcast.144, f32[4,256]{1,0:T(4,128)S(1)} %fusion.16, f32[4,256]{1,0:T(4,128)S(1)} %log_add_fusion, pred[256,3328]{0,1:T(8,128)(4,1)} %bitcast_and_fusion, bf16[3328,256]{1,0:T(8,128)(2,1)S(1)} %bitcast.139), kind=kOutput, calls=%fused_computation.4 | convolution fusion | flops 892862464 | bytes 22421504 | tf_op jit(solution)/shard_map/tgd,sd->gts/dot_general | solution.py:45
  52.1 2.4 %fusion.6 = bf16[3328,128]{0,1:T(8,128)(2,1)S(1)} fusion(bf16[4,256,3328]{1,2,0:T(8,128)(2,1)S(1)} %fusion.2, bf16[256,4,64]{2,0,1:T(8,128)(2,1)S(1)} %get-tuple-element.18, bf16[256,4,64]{2,0,1:T(8,128)(2,1)S(1)} %get-tuple-element.17), kind=kOutput, calls=%fused_computation.17 | convolution fusion | flops 873365504 | bytes 7929856 | tf_op jit(solution)/shard_map/gts,tgd->sd/dot_general | solution.py:45
  55.0 1.4 fusion.12
  56.4 1.7 copy.82
  58.3 1.4 fusion.10
  59.7 1.2 fusion.63
  60.9 1.3 copy.84
  62.4 1.4 bitcast_convert_fusion
  63.8 1.8 copy.85
  65.6 6.0 %convolution_bitcast_fusion.2 = f32[256,4,128]{2,0,1:T(8,128)S(1)} fusion(bf16[4,256,3328]{1,2,0:T(8,128)(2,1)} %copy-done.1, bf16[3328,256]{1,0:T(8,128)(2,1)} %bitcast.138), kind=kOutput, calls=%fused_computation.48 | convolution fusion | flops 872415232 | bytes 8192000 | tf_op jit(solution)/shard_map/gts,sd->tgd/dot_general | solution.py:45
  72.7 1.2 copy.78
  73.9 3.1 %add_convert_fusion = bf16[8,256,256]{1,2,0:T(8,128)(2,1)} fusion(f32[8,256,256]{1,2,0:T(8,128)} %copy.85, bf16[8,256,256]{1,2,0:T(8,128)(2,1)} %collective-permute-done.1), kind=kLoop, calls=%fused_computation.39 | loop fusion | flops 1572864 | bytes 4194304 | tf_op jit(solution)/shard_map/convert_element_type | solution.py:101
  77.1 4.5 %all-to-all-start.1 = ((bf16[8,256,256]{1,2,0:T(8,128)(2,1)}), bf16[8,256,256]{1,2,0:T(8,128)(2,1)}, u32[]{:S(2)}, u32[]{:S(2)}) async-start(bf16[8,256,256]{1,2,0:T(8,128)(2,1)} %add_convert_fusion), calls=%async_computation.1 | async-start | bytes 2097152 | tf_op jit(solution)/shard_map/all_to_all | solution.py:105
  83.1 1.2 copy-done.2
  84.3 2.0 %copy-done.3 = f32[512,8,256]{2,0,1:T(8,128)} copy-done((f32[512,8,256]{2,0,1:T(8,128)}, f32[512,8,256]{2,0,1:T(8,128)S(1)}, u32[]{:S(2)}) %copy-start.3) | copy-done | bytes 4194328
  86.3 1.9 %fusion.8 = bf16[8,256,512]{1,2,0:T(8,128)(2,1)} fusion(f32[512,8,256]{2,0,1:T(8,128)S(1)} %fusion.21, f32[512,8,256]{2,0,1:T(8,128)S(1)} %fusion.19, pred[]{:T(512)S(6)} %eq.63), kind=kLoop, calls=%fused_computation.31 | loop fusion | flops 1048576 | bytes 10485761 | tf_op jit(solution)/shard_map/jit(_where)/select_n | solution.py:176
  88.2 9.1 %all-to-all-done.1 = bf16[8,256,256]{1,2,0:T(8,128)(2,1)} async-done(((bf16[8,256,256]{1,2,0:T(8,128)(2,1)}), bf16[8,256,256]{1,2,0:T(8,128)(2,1)}, u32[]{:S(2)}, u32[]{:S(2)}) %all-to-all-start.1) | async-done | bytes 1048608 | tf_op jit(solution)/shard_map/all_to_all | solution.py:105
  97.3 1.5 convert_reduce_fusion.1
  99.2 1.7 fusion.18
  101.4 1.3 copy-done.4
  103.2 1.1 copy-done.9
  104.3 1.9 %pad_maximum_fusion = bf16[8,256,768]{1,2,0:T(8,128)(2,1)} fusion(bf16[8,256,256]{1,2,0:T(8,128)(2,1)S(1)} %fusion.17, bf16[8,256,512]{1,2,0:T(8,128)(2,1)S(1)} %copy-done.9), kind=kLoop, calls=%fused_computation.30 | loop fusion | flops 6291456 | bytes 6291456 | tf_op jit(solution)/shard_map/concatenate | solution.py:194
  107.0 1.4 copy-done.10
  108.4 1.3 convolution_add_fusion
  110.5 1.5 copy.115
  112.0 4.8 %all-to-all-start.2 = ((bf16[8,512,256]{1,2,0:T(8,128)(2,1)}), bf16[8,512,256]{1,2,0:T(8,128)(2,1)}, u32[]{:S(2)}, u32[]{:S(2)}) async-start(bf16[8,512,256]{1,2,0:T(8,128)(2,1)} %bitcast.129), calls=%async_computation.2 | async-start | bytes 4194304 | tf_op jit(solution)/shard_map/all_to_all | solution.py:105
  116.9 2.9 %select_bitcast_fusion = f32[8,256,512]{1,2,0:T(8,128)S(1)} fusion(f32[512,8,256]{2,0,1:T(8,128)} %copy-done.2, f32[512,8,256]{2,0,1:T(8,128)} %copy-done.3, pred[]{:T(512)S(6)} %eq.63), kind=kLoop, calls=%fused_computation.28 | loop fusion | flops 1048576 | bytes 12582913 | tf_op jit(solution)/shard_map/jit(_where)/select_n | solution.py:176
  120.0 4.5 %fusion.4 = bf16[8,256,768]{1,2,0:T(8,128)(2,1)} fusion(f32[8,256,256]{1,2,0:T(8,128)S(1)} %select_bitcast_fusion.1, f32[8,256,512]{1,2,0:T(8,128)S(1)} %select_bitcast_fusion, bf16[8,256,768]{1,2,0:T(8,128)(2,1)} %collective-permute-done.2), kind=kLoop, calls=%fused_computation.10 | loop fusion | flops 6291456 | bytes 12582912 | tf_op jit(solution)/shard_map/convert_element_type | solution.py:101
  124.6 17.9 %all-to-all-done.2 = bf16[8,512,256]{1,2,0:T(8,128)(2,1)} async-done(((bf16[8,512,256]{1,2,0:T(8,128)(2,1)}), bf16[8,512,256]{1,2,0:T(8,128)(2,1)}, u32[]{:S(2)}, u32[]{:S(2)}) %all-to-all-start.2) | async-done | bytes 2097184 | tf_op jit(solution)/shard_map/all_to_all | solution.py:105
  142.5 5.8 %all-to-all-start.3 = ((bf16[8,256,768]{1,2,0:T(8,128)(2,1)}), bf16[8,256,768]{1,2,0:T(8,128)(2,1)}, u32[]{:S(2)}, u32[]{:S(2)}) async-start(bf16[8,256,768]{1,2,0:T(8,128)(2,1)} %fusion.4), calls=%async_computation.3 | async-start | bytes 6291456 | tf_op jit(solution)/shard_map/all_to_all | solution.py:105
  148.3 2.7 %reduce_sum.51 = bf16[512,256]{0,1:T(8,128)(2,1)} reduce(bf16[8,512,256]{1,2,0:T(8,128)(2,1)} %all-to-all-done.2, bf16[]{:T(256)} %constant.216.clone.1), dimensions={0}, to_apply=%region_4.6 | reduce | flops 917504 | bytes 2359298 | tf_op jit(solution)/shard_map/reduce_sum | solution.py:106
  150.9 35.0 %all-to-all-done.3 = bf16[8,256,768]{1,2,0:T(8,128)(2,1)} async-done(((bf16[8,256,768]{1,2,0:T(8,128)(2,1)}), bf16[8,256,768]{1,2,0:T(8,128)(2,1)}, u32[]{:S(2)}, u32[]{:S(2)}) %all-to-all-start.3) | async-done | bytes 3145760 | tf_op jit(solution)/shard_map/all_to_all | solution.py:105
  185.9 2.4 %convert_reduce_fusion = f32[256,768]{0,1:T(8,128)S(1)} fusion(bf16[8,256,768]{1,2,0:T(8,128)(2,1)} %all-to-all-done.3), kind=kLoop, calls=%fused_computation.11 | loop fusion | flops 2949120 | bytes 3932160 | tf_op jit(solution)/shard_map/reduce_sum | solution.py:106
  188.3 1.0 copy.90
  (88 shorter events, 13.5 us)
Async XLA Ops:
  0.6 3.7 %copy-start = (bf16[4096,128]{1,0:T(8,128)(2,1)S(1)}, bf16[4096,128]{1,0:T(8,128)(2,1)}, u32[]{:S(2)}) copy-start(bf16[4096,128]{1,0:T(8,128)(2,1)} %param.11) | copy-start | bytes 3145732
  0.6 3.7 %copy-start.6 = (bf16[256,4096]{1,0:T(8,128)(2,1)S(1)}, bf16[256,4096]{1,0:T(8,128)(2,1)}, u32[]{:S(2)}) copy-start(bf16[256,4096]{1,0:T(8,128)(2,1)} %param.9) | copy-start | bytes 6291460
  6.6 23.8 %all-to-all-start = ((bf16[8,256,256]{2,1,0:T(8,128)(2,1)}), bf16[8,256,256]{2,1,0:T(8,128)(2,1)}, u32[]{:S(2)}, u32[]{:S(2)}) async-start(bf16[8,256,256]{2,1,0:T(8,128)(2,1)} %broadcast_in_dim.111), calls=%async_computation | async-start | bytes 2097152 | tf_op jit(solution)/shard_map/all_to_all | solution.py:93
  17.2 5.5 %copy-start.17 = (s32[2,32]{1,0:T(2,128)S(1)}, s32[2,32]{1,0:T(2,128)}, u32[]{:S(2)}) copy-start(s32[2,32]{1,0:T(2,128)} %param.14) | copy-start | bytes 772
  17.2 6.6 %copy-start.16 = (bf16[256,512]{1,0:T(8,128)(2,1)S(1)}, bf16[256,512]{1,0:T(8,128)(2,1)}, u32[]{:S(2)}) copy-start(bf16[256,512]{1,0:T(8,128)(2,1)} %param.15) | copy-start | bytes 786436
  30.5 2.9 %collective-permute-start = (bf16[8,256,256]{2,1,0:T(8,128)(2,1)}, bf16[8,256,256]{2,1,0:T(8,128)(2,1)S(1)}, u32[]{:S(2)}, u32[]{:S(2)}) collective-permute-start(bf16[8,256,256]{2,1,0:T(8,128)(2,1)} %all-to-all-done), channel_id=1, source_target_pairs={{0,8},{8,0},{1,9},{9,1},{2,10},{10,2},{3,11},{11,3},{4,12},{12,4},... | collective-permute-start | bytes 3145736 | tf_op jit(solution)/shard_map/ppermute | solution.py:94
  33.3 2.2 %copy-start.14 = (pred[256,3328]{0,1:T(8,128)(4,1)S(1)}, pred[256,3328]{0,1:T(8,128)(4,1)}, u32[]{:S(2)}) copy-start(pred[256,3328]{0,1:T(8,128)(4,1)} %bitcast_and_fusion) | copy-start | bytes 2555908
  35.5 2.5 %copy-start.12 = (bf16[13,256,256]{2,1,0:T(8,128)(2,1)}, bf16[13,256,256]{2,1,0:T(8,128)(2,1)S(1)}, u32[]{:S(2)}) copy-start(bf16[13,256,256]{2,1,0:T(8,128)(2,1)S(1)} %pad_maximum_fusion.1) | copy-start | bytes 5111812
  39.7 3.9 %copy-start.15 = (pred[256,3328]{0,1:T(8,128)(4,1)S(1)}, pred[256,3328]{0,1:T(8,128)(4,1)}, u32[]{:S(2)}) copy-start(pred[256,3328]{0,1:T(8,128)(4,1)} %bitcast_and_fusion) | copy-start | bytes 2555908
  43.6 3.1 %copy-start.13 = (bf16[13,256,256]{2,1,0:T(8,128)(2,1)S(1)}, bf16[13,256,256]{2,1,0:T(8,128)(2,1)}, u32[]{:S(2)}) copy-start(bf16[13,256,256]{2,1,0:T(8,128)(2,1)} %copy-done.12) | copy-start | bytes 5111812
  52.1 2.8 %copy-start.1 = (bf16[4,256,3328]{1,2,0:T(8,128)(2,1)}, bf16[4,256,3328]{1,2,0:T(8,128)(2,1)S(1)}, u32[]{:S(2)}) copy-start(bf16[4,256,3328]{1,2,0:T(8,128)(2,1)S(1)} %fusion.2) | copy-start | bytes 20447236
  62.2 11.7 %collective-permute-start.1 = (bf16[8,256,256]{1,2,0:T(8,128)(2,1)}, bf16[8,256,256]{1,2,0:T(8,128)(2,1)}, u32[]{:S(2)}, u32[]{:S(2)}) collective-permute-start(bf16[8,256,256]{1,2,0:T(8,128)(2,1)} %copy.84), channel_id=1, source_target_pairs={{0,8},{8,0},{1,9},{9,1},{2,10},{10,2},{3,11},{11,3},{4,12},{12,4},... | collective-permute-start | bytes 3145736 | tf_op jit(solution)/shard_map/ppermute | solution.py:100
  72.7 8.9 %copy-start.7 = (bf16[256,4096]{0,1:T(8,128)(2,1)S(1)}, bf16[256,4096]{0,1:T(8,128)(2,1)}, u32[]{:S(2)}) copy-start(bf16[256,4096]{0,1:T(8,128)(2,1)} %copy.87) | copy-start | bytes 6291460
  77.1 20.2 %all-to-all-start.1 = ((bf16[8,256,256]{1,2,0:T(8,128)(2,1)}), bf16[8,256,256]{1,2,0:T(8,128)(2,1)}, u32[]{:S(2)}, u32[]{:S(2)}) async-start(bf16[8,256,256]{1,2,0:T(8,128)(2,1)} %add_convert_fusion), calls=%async_computation.1 | async-start | bytes 2097152 | tf_op jit(solution)/shard_map/all_to_all | solution.py:105
  82.3 1.9 %copy-start.2 = (f32[512,8,256]{2,0,1:T(8,128)}, f32[512,8,256]{2,0,1:T(8,128)S(1)}, u32[]{:S(2)}) copy-start(f32[512,8,256]{2,0,1:T(8,128)S(1)} %fusion.19) | copy-start | bytes 12582916
  84.3 2.0 %copy-start.3 = (f32[512,8,256]{2,0,1:T(8,128)}, f32[512,8,256]{2,0,1:T(8,128)S(1)}, u32[]{:S(2)}) copy-start(f32[512,8,256]{2,0,1:T(8,128)S(1)} %fusion.21) | copy-start | bytes 12582916
  97.3 3.6 %copy-start.8 = (bf16[256,4096]{0,1:T(8,128)(2,1)S(1)}, bf16[256,4096]{0,1:T(8,128)(2,1)}, u32[]{:S(2)}) copy-start(bf16[256,4096]{0,1:T(8,128)(2,1)} %copy.87) | copy-start | bytes 6291460
  101.4 1.3 copy-start.4
  102.7 1.6 copy-start.9
  106.2 2.2 %copy-start.10 = (bf16[4096,512]{1,0:T(8,128)(2,1)S(1)}, bf16[4096,512]{1,0:T(8,128)(2,1)}, u32[]{:S(2)}) copy-start(bf16[4096,512]{1,0:T(8,128)(2,1)} %param.10) | copy-start | bytes 12582916
  106.2 13.8 %collective-permute-start.2 = (bf16[8,256,768]{1,2,0:T(8,128)(2,1)}, bf16[8,256,768]{1,2,0:T(8,128)(2,1)}, u32[]{:S(2)}, u32[]{:S(2)}) collective-permute-start(bf16[8,256,768]{1,2,0:T(8,128)(2,1)} %pad_maximum_fusion), channel_id=1, source_target_pairs={{0,8},{8,0},{1,9},{9,1},{2,10},{10,2},{3,11},{11,3},{4,12},{12,4},... | collective-permute-start | bytes 9437192 | tf_op jit(solution)/shard_map/ppermute | solution.py:100
  108.4 1.4 copy-start.11
  112.0 30.5 %all-to-all-start.2 = ((bf16[8,512,256]{1,2,0:T(8,128)(2,1)}), bf16[8,512,256]{1,2,0:T(8,128)(2,1)}, u32[]{:S(2)}, u32[]{:S(2)}) async-start(bf16[8,512,256]{1,2,0:T(8,128)(2,1)} %bitcast.129), calls=%async_computation.2 | async-start | bytes 4194304 | tf_op jit(solution)/shard_map/all_to_all | solution.py:105
  116.8 2.9 %copy-start.5 = (f32[256,8,256]{2,0,1:T(8,128)S(1)}, f32[256,8,256]{2,0,1:T(8,128)}, u32[]{:S(2)}) copy-start(f32[256,8,256]{2,0,1:T(8,128)} %copy-done.4) | copy-start | bytes 6291460
  142.5 43.4 %all-to-all-start.3 = ((bf16[8,256,768]{1,2,0:T(8,128)(2,1)}), bf16[8,256,768]{1,2,0:T(8,128)(2,1)}, u32[]{:S(2)}, u32[]{:S(2)}) async-start(bf16[8,256,768]{1,2,0:T(8,128)(2,1)} %fusion.4), calls=%async_computation.3 | async-start | bytes 6291456 | tf_op jit(solution)/shard_map/all_to_all | solution.py:105

commit v4 on v2

--- a/solution.py
+++ b/solution.py
@@ -177,7 +177,8 @@
 
     kv_total = scatter_sum(pair_sum(kv_terms[0], kv_terms[1]), ("seq_x", "seq_z"))
     wq_keep, wq_send = weight_halves(query_grad)
-    grad_wq = scatter_sum(pair_sum(wq_keep, wq_send), ("seq_x", "seq_z"))
+    kv_total, wq_terms = lax.optimization_barrier((kv_total, pair_sum(wq_keep, wq_send)))
+    grad_wq = scatter_sum(wq_terms, ("seq_x", "seq_z"))
 
     def weight_terms(grads):
         keep, send = weight_halves(grads)
@@ -189,6 +190,7 @@
     )
     key_grad = rotate(kv_total[:, :HEAD], positions, -1.0).astype(jnp.bfloat16)
     value_grad = kv_total[:, HEAD:].astype(jnp.bfloat16)
+    grad_wq, key_grad, value_grad = lax.optimization_barrier((grad_wq, key_grad, value_grad))
     kv_grad = jnp.concatenate([key_grad, value_grad], axis=1)
     grad_wkv = weight_terms(kv_grad)
     grad_wk = grad_wkv[:, :HEAD]

time: 190 us -> 199 us (1.047)
  blocking collectives: 0 us -> 21.3 us
  waiting for transfers between devices: 71 us -> 57.8 us
  matrix products: 35.5 us -> 38.2 us
  starting transfers between devices: 27.5 us -> 25 us
    all_to_all x0 -> x1, blocking collectives: none -> 21.3 us  [scatter_sum(): arrived = lax.all_to_all(parts, axis, 0, 0, tiled=True)]
    all_to_all x4 -> x3, waiting for transfers between devices: 62.8 us -> 49.7 us  [scatter_sum(): arrived = lax.all_to_all(parts, axis, 0, 0, tiled=True)]
    dot_general x2, matrix products: 1.21 us -> 4.4 us  [weight_halves(): lax.dot_general(normed_even, grads, tokens_first, preferred_element_type=...]
    dot_general x6, matrix products: 22.7 us -> 19.9 us  [product(): return jnp.einsum(form, left, right, preferred_element_type=jnp.float32)]
    all_to_all x4 -> x3, starting transfers between devices: 18.9 us -> 16.5 us  [scatter_sum(): arrived = lax.all_to_all(parts, axis, 0, 0, tiled=True)]
    unnamed x41 -> x35, local copies, waits for them, and re-layouts: 9.98 us -> 8.12 us
  transfers between devices with their start and end apart: 9 -> 8, of which waited for: 7 -> 6; matrix products, arithmetic and copies ran while one was open for 24% -> 17% of each run, Pallas kernels for 0% -> 0%
where the time goes in v4:
time: 199 us; the launch traced here: 198 us
  waiting for transfers between devices  57.8 us (29%)
  matrix products  38.2 us (19%)
  other arithmetic  32 us (16%)
  starting transfers between devices  25 us (13%)
  local copies, waits for them, and re-layouts  22.7 us (11%)
  blocking collectives  21.3 us (11%)
    all_to_all x3, waiting for transfers between devices, scatter_sum(): arrived = lax.all_to_all(parts, axis, 0, 0, tiled=True)  49.7 us
    all_to_all x1, blocking collectives, scatter_sum(): arrived = lax.all_to_all(parts, axis, 0, 0, tiled=True)  21.3 us
    dot_general x6, matrix products, product(): return jnp.einsum(form, left, right, preferred_element_type=jnp.float32)  19.9 us
    all_to_all x3, starting transfers between devices, scatter_sum(): arrived = lax.all_to_all(parts, axis, 0, 0, tiled=True)  16.5 us
    unnamed x35, local copies, waits for them, and re-layouts  8.12 us
    convert_element_type x3, other arithmetic, pair_sum(): (keep.astype(jnp.float32) + got.astype(jnp.float32)).astype(jnp.bfloat16)  8 us
    all_to_all x1, starting transfers between devices, gather_rows(): mine = lax.all_to_all(copies, ('seq_x', 'seq_z'), 0, 0, tiled=True)  7.86 us
    reduce_sum x4, other arithmetic, scatter_sum(): return jnp.sum(arrived.astype(jnp.float32), axis=0)  4.75 us
  transfers between devices with their start and end apart: 8, of which 6 were waited for; matrix products, arithmetic and copies ran while one was open for 17% of the time, Pallas kernels for 0%

profile of v4, /device:TPU:0, one launch (start us, length us, event | category | flops | bytes accessed | tf_op | source)
XLA Modules:
  0.0 198.3 jit_solution(13285845585608695494)
XLA Ops:
  1.5 2.8 %convolution_convert_fusion = bf16[256,128]{0,1:T(8,128)(2,1)S(1)} fusion(bf16[256,4096]{1,0:T(8,128)(2,1)} %param.9, bf16[4096,128]{1,0:T(8,128)(2,1)} %param.12), kind=kOutput, calls=%fused_computation.51 | convolution fusion | flops 268468224 | bytes 3211264 | tf_op jit(solution)/shard_map/dot_general | solution.py:124
  5.6 1.1 broadcast_in_dim.111
  6.7 7.9 %all-to-all-start = ((bf16[8,256,256]{2,1,0:T(8,128)(2,1)}), bf16[8,256,256]{2,1,0:T(8,128)(2,1)}, u32[]{:S(2)}, u32[]{:S(2)}) async-start(bf16[8,256,256]{2,1,0:T(8,128)(2,1)} %broadcast_in_dim.111), calls=%async_computation | async-start | bytes 2097152 | tf_op jit(solution)/shard_map/all_to_all | solution.py:93
  14.6 2.6 %copy.86 = bf16[256,4096]{0,1:T(8,128)(2,1)} copy(bf16[256,4096]{1,0:T(8,128)(2,1)S(1)} %copy-done.2) | data formatting | bytes 4194304 | tf_op args[0]
  17.2 4.3 %fusion.67 = f32[256,512]{1,0:T(8,128)} fusion(bf16[256,4096]{1,0:T(8,128)(2,1)S(1)} %copy-done.2, bf16[4096,512]{1,0:T(8,128)(2,1)} %param.10), kind=kOutput, calls=%fused_computation.161 | convolution fusion | flops 1073741824 | bytes 6815744 | tf_op jit(solution)/shard_map/dot_general | solution.py:119
  21.4 1.2 reshape.435
  24.0 1.9 bitcast_and_fusion
  25.9 4.6 %all-to-all-done = bf16[8,256,256]{2,1,0:T(8,128)(2,1)} async-done(((bf16[8,256,256]{2,1,0:T(8,128)(2,1)}), bf16[8,256,256]{2,1,0:T(8,128)(2,1)}, u32[]{:S(2)}, u32[]{:S(2)}) %all-to-all-start) | async-done | bytes 1048608 | tf_op jit(solution)/shard_map/all_to_all | solution.py:93
  31.6 0.9 dynamic-slice_bitcast_fusion
  33.3 2.0 %fusion.15 = bf16[2,3,2,256,256]{4,3,2,1,0:T(8,128)(2,1)S(1)} fusion(s32[]{:T(128)S(6)} %select_n.303, bf16[1,4,2,256,256]{4,3,2,1,0:T(8,128)(2,1)} %bitcast.4, bf16[1,4,2,256,256]{4,3,2,1,0:T(8,128)(2,1)S(1)} %bitcast.145), kind=kLoop, calls=%fused_computation.45 | loop fusion | flops 2359296 | bytes 3670020 | tf_op jit(solution)/shard_map/jit(_roll_dynamic)/concatenate | solution.py:133
  35.5 2.4 %fusion.66 = (f32[4,256]{1,0:T(4,128)S(1)}, f32[4,256,3328]{1,2,0:T(8,128)S(1)}) fusion(bf16[256,4,64]{2,0,1:T(8,128)(2,1)S(1)} %get-tuple-element.28, bf16[256,4,64]{2,0,1:T(8,128)(2,1)S(1)} %get-tuple-element.27, bf16[3328,256]{1,0:T(8,128)(2,1)S(1)} %bitcast.141, pred[256,3328]{0,1:T(8,128)(4,1)S(1)} %copy-done.9), kind=kOutput, calls=%fused_computation.160 | convolution fusion | flops 883162112 | bytes 15863808 | tf_op jit(solution)/shard_map/tgd,sd->gts/dot_general | solution.py:45
  38.0 1.8 exponential_reduce_fusion
  39.8 3.9 %fusion.17 = f32[4,256]{1,0:T(4,128)S(1)} fusion(bf16[3328,256]{1,0:T(8,128)(2,1)} %bitcast.142, f32[4,256,3328]{1,2,0:T(8,128)S(1)} %get-tuple-element.43, f32[4,256]{1,0:T(4,128)S(1)} %log_add_fusion, pred[256,3328]{0,1:T(8,128)(4,1)} %bitcast_and_fusion, bf16[256,4,128]{0,2,1:T(8,128)(2,1)S(1)} %bitcast.147), kind=kOutput, calls=%fused_computation.49 | convolution fusion | flops 883031040 | bytes 15605760 | tf_op jit(solution)/shard_map/gts,sd->gtd/dot_general | solution.py:45
  43.7 3.1 %fusion.6 = bf16[3328,128]{0,1:T(8,128)(2,1)S(1)} fusion(bf16[256,4,128]{0,2,1:T(8,128)(2,1)S(1)} %bitcast.148, f32[4,256,3328]{1,2,0:T(8,128)S(1)} %get-tuple-element.43, f32[4,256]{1,0:T(4,128)S(1)} %log_add_fusion, pred[256,3328]{0,1:T(8,128)(4,1)S(1)} %copy-done.10), kind=kOutput, calls=%fused_computation.15 | convolution fusion | flops 883064832 | bytes 15601664 | tf_op jit(solution)/shard_map/gts,tgd->sd/dot_general | solution.py:45
  46.8 5.4 %fusion.2 = bf16[4,256,3328]{1,2,0:T(8,128)(2,1)S(1)} fusion(f32[4,256,3328]{1,2,0:T(8,128)S(1)} %get-tuple-element.43, bf16[256,4,128]{0,2,1:T(8,128)(2,1)S(1)} %bitcast.149, f32[4,256]{1,0:T(4,128)S(1)} %fusion.17, f32[4,256]{1,0:T(4,128)S(1)} %log_add_fusion, pred[256,3328]{0,1:T(8,128)(4,1)} %bitcast_and_fusion, bf16[3328,256]{1,0:T(8,128)(2,1)S(1)} %bitcast.143), kind=kOutput, calls=%fused_computation.4 | convolution fusion | flops 892862464 | bytes 22421504 | tf_op jit(solution)/shard_map/tgd,sd->gts/dot_general | solution.py:45
  52.2 2.4 %fusion.5 = bf16[3328,128]{0,1:T(8,128)(2,1)S(1)} fusion(bf16[4,256,3328]{1,2,0:T(8,128)(2,1)S(1)} %fusion.2, bf16[256,4,64]{2,0,1:T(8,128)(2,1)S(1)} %get-tuple-element.28, bf16[256,4,64]{2,0,1:T(8,128)(2,1)S(1)} %get-tuple-element.27), kind=kOutput, calls=%fused_computation.14 | convolution fusion | flops 873365504 | bytes 7929856 | tf_op jit(solution)/shard_map/gts,tgd->sd/dot_general | solution.py:45
  54.6 1.4 fusion.13
  56.0 2.7 %convolution_bitcast_fusion.2 = f32[256,4,128]{2,0,1:T(8,128)S(1)} fusion(bf16[4,256,3328]{1,2,0:T(8,128)(2,1)S(1)} %fusion.2, bf16[3328,256]{1,0:T(8,128)(2,1)S(1)} %bitcast.144), kind=kOutput, calls=%fused_computation.48 | convolution fusion | flops 872415232 | bytes 8192000 | tf_op jit(solution)/shard_map/gts,sd->tgd/dot_general | solution.py:45
  59.8 1.1 copy.78
  60.9 2.7 %fusion.22 = f32[512,8,256]{2,0,1:T(8,128)} fusion(bf16[256,512,1]{0,1,2:T(8,128)(2,1)S(1)} %bitcast.138, bf16[256,8,2,256]{0,3,2,1:T(8,128)(2,1)S(1)} %bitcast.130), kind=kOutput, calls=%fused_computation.59 | convolution fusion | flops 536870912 | bytes 5505024 | tf_op jit(solution)/shard_map/dot_general | solution.py:175
  63.7 2.7 %fusion.20 = f32[512,8,256]{2,0,1:T(8,128)} fusion(bf16[256,512,1]{0,1,2:T(8,128)(2,1)S(1)} %bitcast.139, bf16[256,8,2,256]{0,3,2,1:T(8,128)(2,1)S(1)} %bitcast.131), kind=kOutput, calls=%fused_computation.57 | convolution fusion | flops 536870912 | bytes 5505024 | tf_op jit(solution)/shard_map/dot_general | solution.py:174
  66.4 1.7 copy.82
  68.9 1.0 broadcast_select_fusion
  69.9 1.4 fusion.10
  71.4 1.3 copy.84
  72.9 4.1 %fusion.8 = bf16[8,256,512]{1,2,0:T(8,128)(2,1)} fusion(f32[512,8,256]{2,0,1:T(8,128)} %fusion.22, f32[512,8,256]{2,0,1:T(8,128)} %fusion.20, pred[]{:T(512)S(6)} %eq.63), kind=kLoop, calls=%fused_computation.29 | loop fusion | flops 1048576 | bytes 10485761 | tf_op jit(solution)/shard_map/convert_element_type | solution.py:100
  77.3 1.6 bitcast_convert_fusion
  78.9 1.9 copy.85
  80.8 1.6 add_convert_fusion
  82.5 21.3 %all_to_all.25 = bf16[8,256,256]{1,2,0:T(8,128)(2,1)S(1)} all-to-all(bf16[8,256,256]{1,2,0:T(8,128)(2,1)S(1)} %add_convert_fusion), channel_id=1, replica_groups=mesh['seq_x'=2,'seq_z'=4,'seq_core'=2,'kvh_x'=2,'kvh_y'=4] {'seq_x','seq..., dimensions={0} | all-to-all | bytes 2097152 | tf_op jit(solution)/shard_map/all_to_all | solution.py:105
  104.7 4.9 %fusion.7 = bf16[8,256,512]{1,2,0:T(8,128)(2,1)} fusion(bf16[8,256,512]{1,2,0:T(8,128)(2,1)} %collective-permute-done.2, f32[512,8,256]{2,0,1:T(8,128)} %fusion.20, f32[512,8,256]{2,0,1:T(8,128)S(1)} %copy-done.1, pred[]{:T(512)S(6)} %eq.63), kind=kLoop, calls=%fused_computation.25 | loop fusion | flops 4194304 | bytes 12582913 | tf_op jit(solution)/shard_map/convert_element_type | solution.py:101
  109.6 3.6 %all-to-all-start.2 = ((bf16[8,256,512]{1,2,0:T(8,128)(2,1)}), bf16[8,256,512]{1,2,0:T(8,128)(2,1)S(1)}, u32[]{:S(2)}, u32[]{:S(2)}) async-start(bf16[8,256,512]{1,2,0:T(8,128)(2,1)} %fusion.7), calls=%async_computation.2 | async-start | bytes 4194304 | tf_op jit(solution)/shard_map/all_to_all | solution.py:105
  113.2 0.9 slice.144
  114.1 0.9 slice_bitcast_fusion.12
  115.4 21.7 %all-to-all-done.2 = bf16[8,256,512]{1,2,0:T(8,128)(2,1)S(1)} async-done(((bf16[8,256,512]{1,2,0:T(8,128)(2,1)}), bf16[8,256,512]{1,2,0:T(8,128)(2,1)S(1)}, u32[]{:S(2)}, u32[]{:S(2)}) %all-to-all-start.2) | async-done | bytes 2097184 | tf_op jit(solution)/shard_map/all_to_all | solution.py:105
  137.1 1.1 convert_reduce_fusion
  139.0 0.9 copy-done.4
  141.0 1.3 convolution_add_fusion
  143.1 1.5 copy.115
  144.7 4.5 %all-to-all-start.3 = ((bf16[8,512,256]{1,2,0:T(8,128)(2,1)}), bf16[8,512,256]{1,2,0:T(8,128)(2,1)}, u32[]{:S(2)}, u32[]{:S(2)}) async-start(bf16[8,512,256]{1,2,0:T(8,128)(2,1)} %bitcast.134), calls=%async_computation.3 | async-start | bytes 4194304 | tf_op jit(solution)/shard_map/all_to_all | solution.py:105
  149.2 1.7 fusion.19
  151.4 2.6 %collective-permute-done.3 = bf16[8,256,256]{1,2,0:T(8,128)(2,1)S(1)} collective-permute-done((bf16[8,256,256]{1,2,0:T(8,128)(2,1)S(1)}, bf16[8,256,256]{1,2,0:T(8,128)(2,1)S(1)}, u32[]{:S(2)}, u32[]{:S(2)}) %collective-permute-start.3) | collective-permute-done | bytes 1048608 | tf_op jit(solution)/shard_map/ppermute | solution.py:100
  154.0 1.4 fusion.12
  155.5 17.0 %all-to-all-done.3 = bf16[8,512,256]{1,2,0:T(8,128)(2,1)} async-done(((bf16[8,512,256]{1,2,0:T(8,128)(2,1)}), bf16[8,512,256]{1,2,0:T(8,128)(2,1)}, u32[]{:S(2)}, u32[]{:S(2)}) %all-to-all-start.3) | async-done | bytes 2097184 | tf_op jit(solution)/shard_map/all_to_all | solution.py:105
  172.5 8.4 %all-to-all-start.4 = ((bf16[8,256,256]{1,2,0:T(8,128)(2,1)}), bf16[8,256,256]{1,2,0:T(8,128)(2,1)S(1)}, u32[]{:S(2)}, u32[]{:S(2)}) async-start(bf16[8,256,256]{1,2,0:T(8,128)(2,1)} %fusion.12), calls=%async_computation.4 | async-start | bytes 2097152 | tf_op jit(solution)/shard_map/all_to_all | solution.py:105
  180.9 2.0 %copy.90 = f32[256,512]{1,0:T(8,128)} copy(f32[256,512]{0,1:T(8,128)} %convert_reduce_fusion) | data formatting | bytes 1048576
  182.9 2.7 %reduce_sum.61 = bf16[512,256]{0,1:T(8,128)(2,1)} reduce(bf16[8,512,256]{1,2,0:T(8,128)(2,1)} %all-to-all-done.3, bf16[]{:T(256)} %constant.216.clone.1), dimensions={0}, to_apply=%region_5.7 | reduce | flops 917504 | bytes 2359298 | tf_op jit(solution)/shard_map/reduce_sum | solution.py:106
  185.6 11.0 %all-to-all-done.4 = bf16[8,256,256]{1,2,0:T(8,128)(2,1)S(1)} async-done(((bf16[8,256,256]{1,2,0:T(8,128)(2,1)}), bf16[8,256,256]{1,2,0:T(8,128)(2,1)S(1)}, u32[]{:S(2)}, u32[]{:S(2)}) %all-to-all-start.4) | async-done | bytes 1048608 | tf_op jit(solution)/shard_map/all_to_all | solution.py:105
  (79 shorter events, 14.2 us)
Async XLA Ops:
  0.6 3.7 %copy-start = (bf16[4096,128]{1,0:T(8,128)(2,1)S(1)}, bf16[4096,128]{1,0:T(8,128)(2,1)}, u32[]{:S(2)}) copy-start(bf16[4096,128]{1,0:T(8,128)(2,1)} %param.11) | copy-start | bytes 3145732
  0.6 3.7 %copy-start.2 = (bf16[256,4096]{1,0:T(8,128)(2,1)S(1)}, bf16[256,4096]{1,0:T(8,128)(2,1)}, u32[]{:S(2)}) copy-start(bf16[256,4096]{1,0:T(8,128)(2,1)} %param.9) | copy-start | bytes 6291460
  6.7 23.8 %all-to-all-start = ((bf16[8,256,256]{2,1,0:T(8,128)(2,1)}), bf16[8,256,256]{2,1,0:T(8,128)(2,1)}, u32[]{:S(2)}, u32[]{:S(2)}) async-start(bf16[8,256,256]{2,1,0:T(8,128)(2,1)} %broadcast_in_dim.111), calls=%async_computation | async-start | bytes 2097152 | tf_op jit(solution)/shard_map/all_to_all | solution.py:93
  17.2 5.5 %copy-start.12 = (s32[2,32]{1,0:T(2,128)S(1)}, s32[2,32]{1,0:T(2,128)}, u32[]{:S(2)}) copy-start(s32[2,32]{1,0:T(2,128)} %param.14) | copy-start | bytes 772
  17.2 6.6 %copy-start.11 = (bf16[256,512]{1,0:T(8,128)(2,1)S(1)}, bf16[256,512]{1,0:T(8,128)(2,1)}, u32[]{:S(2)}) copy-start(bf16[256,512]{1,0:T(8,128)(2,1)} %param.15) | copy-start | bytes 786436
  30.5 2.9 %collective-permute-start = (bf16[8,256,256]{2,1,0:T(8,128)(2,1)}, bf16[8,256,256]{2,1,0:T(8,128)(2,1)S(1)}, u32[]{:S(2)}, u32[]{:S(2)}) collective-permute-start(bf16[8,256,256]{2,1,0:T(8,128)(2,1)} %all-to-all-done), channel_id=1, source_target_pairs={{0,8},{8,0},{1,9},{9,1},{2,10},{10,2},{3,11},{11,3},{4,12},{12,4},... | collective-permute-start | bytes 3145736 | tf_op jit(solution)/shard_map/ppermute | solution.py:94
  33.3 2.2 %copy-start.9 = (pred[256,3328]{0,1:T(8,128)(4,1)S(1)}, pred[256,3328]{0,1:T(8,128)(4,1)}, u32[]{:S(2)}) copy-start(pred[256,3328]{0,1:T(8,128)(4,1)} %bitcast_and_fusion) | copy-start | bytes 2555908
  35.5 2.5 %copy-start.7 = (bf16[13,256,256]{2,1,0:T(8,128)(2,1)}, bf16[13,256,256]{2,1,0:T(8,128)(2,1)S(1)}, u32[]{:S(2)}) copy-start(bf16[13,256,256]{2,1,0:T(8,128)(2,1)S(1)} %pad_maximum_fusion) | copy-start | bytes 5111812
  39.8 3.9 %copy-start.10 = (pred[256,3328]{0,1:T(8,128)(4,1)S(1)}, pred[256,3328]{0,1:T(8,128)(4,1)}, u32[]{:S(2)}) copy-start(pred[256,3328]{0,1:T(8,128)(4,1)} %bitcast_and_fusion) | copy-start | bytes 2555908
  43.7 3.1 %copy-start.8 = (bf16[13,256,256]{2,1,0:T(8,128)(2,1)S(1)}, bf16[13,256,256]{2,1,0:T(8,128)(2,1)}, u32[]{:S(2)}) copy-start(bf16[13,256,256]{2,1,0:T(8,128)(2,1)} %copy-done.7) | copy-start | bytes 5111812
  58.7 2.2 %copy-start.3 = (bf16[256,4096]{0,1:T(8,128)(2,1)S(1)}, bf16[256,4096]{0,1:T(8,128)(2,1)}, u32[]{:S(2)}) copy-start(bf16[256,4096]{0,1:T(8,128)(2,1)} %copy.86) | copy-start | bytes 6291460
  72.8 8.1 %collective-permute-start.1 = (bf16[8,256,256]{1,2,0:T(8,128)(2,1)}, bf16[8,256,256]{1,2,0:T(8,128)(2,1)}, u32[]{:S(2)}, u32[]{:S(2)}) collective-permute-start(bf16[8,256,256]{1,2,0:T(8,128)(2,1)} %copy.84), channel_id=1, source_target_pairs={{0,8},{8,0},{1,9},{9,1},{2,10},{10,2},{3,11},{11,3},{4,12},{12,4},... | collective-permute-start | bytes 3145736 | tf_op jit(solution)/shard_map/ppermute | solution.py:100
  77.0 27.7 %collective-permute-start.2 = (bf16[8,256,512]{1,2,0:T(8,128)(2,1)}, bf16[8,256,512]{1,2,0:T(8,128)(2,1)}, u32[]{:S(2)}, u32[]{:S(2)}) collective-permute-start(bf16[8,256,512]{1,2,0:T(8,128)(2,1)} %fusion.8), channel_id=1, source_target_pairs={{0,8},{8,0},{1,9},{9,1},{2,10},{10,2},{3,11},{11,3},{4,12},{12,4},... | collective-permute-start | bytes 6291464 | tf_op jit(solution)/shard_map/ppermute | solution.py:100
  80.8 23.8 %copy-start.1 = (f32[512,8,256]{2,0,1:T(8,128)S(1)}, f32[512,8,256]{2,0,1:T(8,128)}, u32[]{:S(2)}) copy-start(f32[512,8,256]{2,0,1:T(8,128)} %fusion.22) | copy-start | bytes 12582916
  109.6 27.5 %all-to-all-start.2 = ((bf16[8,256,512]{1,2,0:T(8,128)(2,1)}), bf16[8,256,512]{1,2,0:T(8,128)(2,1)S(1)}, u32[]{:S(2)}, u32[]{:S(2)}) async-start(bf16[8,256,512]{1,2,0:T(8,128)(2,1)} %fusion.7), calls=%async_computation.2 | async-start | bytes 4194304 | tf_op jit(solution)/shard_map/all_to_all | solution.py:105
  138.2 1.6 copy-start.4
  138.2 2.8 %copy-start.5 = (bf16[4096,512]{1,0:T(8,128)(2,1)S(1)}, bf16[4096,512]{1,0:T(8,128)(2,1)}, u32[]{:S(2)}) copy-start(bf16[4096,512]{1,0:T(8,128)(2,1)} %param.10) | copy-start | bytes 12582916
  141.0 1.4 copy-start.6
  144.7 27.8 %all-to-all-start.3 = ((bf16[8,512,256]{1,2,0:T(8,128)(2,1)}), bf16[8,512,256]{1,2,0:T(8,128)(2,1)}, u32[]{:S(2)}, u32[]{:S(2)}) async-start(bf16[8,512,256]{1,2,0:T(8,128)(2,1)} %bitcast.134), calls=%async_computation.3 | async-start | bytes 4194304 | tf_op jit(solution)/shard_map/all_to_all | solution.py:105
  151.3 2.7 %collective-permute-start.3 = (bf16[8,256,256]{1,2,0:T(8,128)(2,1)S(1)}, bf16[8,256,256]{1,2,0:T(8,128)(2,1)S(1)}, u32[]{:S(2)}, u32[]{:S(2)}) collective-permute-start(bf16[8,256,256]{1,2,0:T(8,128)(2,1)S(1)} %fusion.18), channel_id=1, source_target_pairs={{0,8},{8,0},{1,9},{9,1},{2,10},{10,2},{3,11},{11,3},{4,12},{12,4},... | collective-permute-start | bytes 3145736 | tf_op jit(solution)/shard_map/ppermute | solution.py:100
  172.5 24.1 %all-to-all-start.4 = ((bf16[8,256,256]{1,2,0:T(8,128)(2,1)}), bf16[8,256,256]{1,2,0:T(8,128)(2,1)S(1)}, u32[]{:S(2)}, u32[]{:S(2)}) async-start(bf16[8,256,256]{1,2,0:T(8,128)(2,1)} %fusion.12), calls=%async_computation.4 | async-start | bytes 2097152 | tf_op jit(solution)/shard_map/all_to_all | solution.py:105

commit v5 on v2

--- a/solution.py
+++ b/solution.py
@@ -185,7 +185,7 @@
 
     contract = (((1,), (1,)), ((), ()))
     partial_input = lax.dot_general(
-        w_query, query_grad, contract, preferred_element_type=jnp.float32
+        query_grad, w_query, contract, preferred_element_type=jnp.float32
     )
     key_grad = rotate(kv_total[:, :HEAD], positions, -1.0).astype(jnp.bfloat16)
     value_grad = kv_total[:, HEAD:].astype(jnp.bfloat16)
@@ -194,14 +194,15 @@
     grad_wk = grad_wkv[:, :HEAD]
     grad_wv = grad_wkv[:, HEAD:]
     partial_input = partial_input + lax.dot_general(
-        w_key, key_grad, contract, preferred_element_type=jnp.float32
+        key_grad, w_key, contract, preferred_element_type=jnp.float32
     )
     partial_input = partial_input + lax.dot_general(
-        w_value, value_grad, contract, preferred_element_type=jnp.float32
-    )
-    feat = partial_input.shape[0] // kvh_count
-    input_terms = partial_input.astype(jnp.bfloat16).reshape(kvh_count, feat, tok_rows)
-    grad_normed = scatter_sum(input_terms, KVH_AXES).T.astype(jnp.bfloat16)
+        value_grad, w_value, contract, preferred_element_type=jnp.float32
+    )
+    feat = partial_input.shape[1] // kvh_count
+    input_terms = partial_input.astype(jnp.bfloat16).reshape(tok_rows, kvh_count, feat)
+    arrived = lax.all_to_all(input_terms, KVH_AXES, 1, 1, tiled=True)
+    grad_normed = jnp.sum(arrived.astype(jnp.float32), axis=1).astype(jnp.bfloat16)
     return (grad_normed, grad_wq, grad_wk, grad_wv)
 
 

time: 190 us -> 190 us (level)
    all_to_all x0 -> x1, waiting for transfers between devices: none -> 20.1 us  [body(): arrived = lax.all_to_all(input_terms, KVH_AXES, 1, 1, tiled=True)]
    all_to_all x4 -> x3, waiting for transfers between devices: 62.8 us -> 42.8 us  [scatter_sum(): arrived = lax.all_to_all(parts, axis, 0, 0, tiled=True)]
    all_to_all x0 -> x1, starting transfers between devices: none -> 4.81 us  [body(): arrived = lax.all_to_all(input_terms, KVH_AXES, 1, 1, tiled=True)]
    all_to_all x4 -> x3, starting transfers between devices: 18.9 us -> 14.1 us  [scatter_sum(): arrived = lax.all_to_all(parts, axis, 0, 0, tiled=True)]
    reduce_sum x0 -> x1, other arithmetic: none -> 2.66 us  [body(): jnp.sum(arrived.astype(jnp.float32), axis=1).astype(jnp.bfloat16)]
    reduce_sum x4 -> x3, other arithmetic: 6.52 us -> 3.86 us  [scatter_sum(): return jnp.sum(arrived.astype(jnp.float32), axis=0)]
where the time goes in v5:
time: 190 us; the launch traced here: 189 us
  waiting for transfers between devices  71 us (37%)
  matrix products  35.5 us (19%)
  other arithmetic  32 us (17%)
  starting transfers between devices  27.5 us (14%)
  local copies, waits for them, and re-layouts  22.2 us (12%)
    all_to_all x3, waiting for transfers between devices, scatter_sum(): arrived = lax.all_to_all(parts, axis, 0, 0, tiled=True)  42.8 us
    dot_general x6, matrix products, product(): return jnp.einsum(form, left, right, preferred_element_type=jnp.float32)  22.7 us
    all_to_all x1, waiting for transfers between devices, body(): arrived = lax.all_to_all(input_terms, KVH_AXES, 1, 1, tiled=True)  20.1 us
    all_to_all x3, starting transfers between devices, scatter_sum(): arrived = lax.all_to_all(parts, axis, 0, 0, tiled=True)  14.1 us
    unnamed x41, local copies, waits for them, and re-layouts  9.98 us
    convert_element_type x3, other arithmetic, pair_sum(): (keep.astype(jnp.float32) + got.astype(jnp.float32)).astype(jnp.bfloat16)  9.56 us
    all_to_all x1, starting transfers between devices, gather_rows(): mine = lax.all_to_all(copies, ('seq_x', 'seq_z'), 0, 0, tiled=True)  7.99 us
    all_to_all x1, starting transfers between devices, body(): arrived = lax.all_to_all(input_terms, KVH_AXES, 1, 1, tiled=True)  4.81 us
  transfers between devices with their start and end apart: 9, of which 7 were waited for; matrix products, arithmetic and copies ran while one was open for 24% of the time, Pallas kernels for 0%

profile of v5, /device:TPU:0, one launch (start us, length us, event | category | flops | bytes accessed | tf_op | source)
XLA Modules:
  0.0 189.4 jit_solution(9433695560567495777)
XLA Ops:
  1.9 2.4 %convolution_bitcast_fusion.3 = f32[256,1,128]{0,2,1:T(8,128)S(1)} fusion(bf16[256,4096]{1,0:T(8,128)(2,1)} %param.9, bf16[4096,128]{1,0:T(8,128)(2,1)S(1)} %copy-done), kind=kOutput, calls=%fused_computation.50 | convolution fusion | flops 268435456 | bytes 3276800 | tf_op jit(solution)/shard_map/dot_general | solution.py:122
  4.4 0.8 convolution_convert_fusion
  5.7 1.0 broadcast_in_dim.111
  6.7 8.0 %all-to-all-start = ((bf16[8,256,256]{2,1,0:T(8,128)(2,1)}), bf16[8,256,256]{2,1,0:T(8,128)(2,1)}, u32[]{:S(2)}, u32[]{:S(2)}) async-start(bf16[8,256,256]{2,1,0:T(8,128)(2,1)} %broadcast_in_dim.111), calls=%async_computation | async-start | bytes 2097152 | tf_op jit(solution)/shard_map/all_to_all | solution.py:93
  14.8 2.5 %copy.87 = bf16[256,4096]{0,1:T(8,128)(2,1)} copy(bf16[256,4096]{1,0:T(8,128)(2,1)S(1)} %copy-done.4) | data formatting | bytes 4194304 | tf_op args[0]
  18.4 4.3 %fusion.69 = f32[256,512]{1,0:T(8,128)} fusion(bf16[256,4096]{1,0:T(8,128)(2,1)S(1)} %copy-done.4, bf16[4096,512]{1,0:T(8,128)(2,1)} %param.10), kind=kOutput, calls=%fused_computation.163 | convolution fusion | flops 1073741824 | bytes 6815744 | tf_op jit(solution)/shard_map/dot_general | solution.py:119
  22.7 1.2 reshape.435
  24.1 1.8 bitcast_and_fusion
  26.0 4.7 %all-to-all-done = bf16[8,256,256]{2,1,0:T(8,128)(2,1)} async-done(((bf16[8,256,256]{2,1,0:T(8,128)(2,1)}), bf16[8,256,256]{2,1,0:T(8,128)(2,1)}, u32[]{:S(2)}, u32[]{:S(2)}) %all-to-all-start) | async-done | bytes 1048608 | tf_op jit(solution)/shard_map/all_to_all | solution.py:93
  31.8 0.9 dynamic-slice_bitcast_fusion
  32.7 0.8 collective-permute-done
  33.5 2.0 %fusion.15 = bf16[2,3,2,256,256]{4,3,2,1,0:T(8,128)(2,1)S(1)} fusion(s32[]{:T(128)S(6)} %select_n.303, bf16[1,4,2,256,256]{4,3,2,1,0:T(8,128)(2,1)} %bitcast.4, bf16[1,4,2,256,256]{4,3,2,1,0:T(8,128)(2,1)S(1)} %bitcast.142), kind=kLoop, calls=%fused_computation.45 | loop fusion | flops 2359296 | bytes 3670020 | tf_op jit(solution)/shard_map/jit(_roll_dynamic)/concatenate | solution.py:133
  35.7 2.4 %fusion.67 = (f32[4,256]{1,0:T(4,128)S(1)}, f32[4,256,3328]{1,2,0:T(8,128)S(1)}) fusion(bf16[256,4,64]{2,0,1:T(8,128)(2,1)S(1)} %get-tuple-element.18, bf16[256,4,64]{2,0,1:T(8,128)(2,1)S(1)} %get-tuple-element.17, bf16[3328,256]{1,0:T(8,128)(2,1)S(1)} %bitcast.138, pred[256,3328]{0,1:T(8,128)(4,1)S(1)} %copy-done.12), kind=kOutput, calls=%fused_computation.161 | convolution fusion | flops 883162112 | bytes 15863808 | tf_op jit(solution)/shard_map/tgd,sd->gts/dot_general | solution.py:45
  38.1 1.8 exponential_reduce_fusion
  40.0 4.2 %fusion.6 = bf16[3328,128]{0,1:T(8,128)(2,1)S(1)} fusion(bf16[256,4,128]{0,2,1:T(8,128)(2,1)S(1)} %bitcast.143, f32[4,256,3328]{1,2,0:T(8,128)S(1)} %get-tuple-element.33, f32[4,256]{1,0:T(4,128)S(1)} %log_add_fusion, pred[256,3328]{0,1:T(8,128)(4,1)} %bitcast_and_fusion), kind=kOutput, calls=%fused_computation.15 | convolution fusion | flops 883064832 | bytes 15601664 | tf_op jit(solution)/shard_map/gts,tgd->sd/dot_general | solution.py:45
  44.2 2.4 %fusion.17 = f32[4,256]{1,0:T(4,128)S(1)} fusion(bf16[3328,256]{1,0:T(8,128)(2,1)S(1)} %bitcast.140, f32[4,256,3328]{1,2,0:T(8,128)S(1)} %get-tuple-element.33, f32[4,256]{1,0:T(4,128)S(1)} %log_add_fusion, pred[256,3328]{0,1:T(8,128)(4,1)S(1)} %copy-done.13, bf16[256,4,128]{0,2,1:T(8,128)(2,1)S(1)} %bitcast.144), kind=kOutput, calls=%fused_computation.49 | convolution fusion | flops 883031040 | bytes 15605760 | tf_op jit(solution)/shard_map/gts,sd->gtd/dot_general | solution.py:45
  46.6 5.4 %fusion.2 = bf16[4,256,3328]{1,2,0:T(8,128)(2,1)S(1)} fusion(f32[4,256,3328]{1,2,0:T(8,128)S(1)} %get-tuple-element.33, bf16[256,4,128]{0,2,1:T(8,128)(2,1)S(1)} %bitcast.145, f32[4,256]{1,0:T(4,128)S(1)} %fusion.17, f32[4,256]{1,0:T(4,128)S(1)} %log_add_fusion, pred[256,3328]{0,1:T(8,128)(4,1)} %bitcast_and_fusion, bf16[3328,256]{1,0:T(8,128)(2,1)S(1)} %bitcast.141), kind=kOutput, calls=%fused_computation.4 | convolution fusion | flops 892862464 | bytes 22421504 | tf_op jit(solution)/shard_map/tgd,sd->gts/dot_general | solution.py:45
  52.0 2.4 %fusion.5 = bf16[3328,128]{0,1:T(8,128)(2,1)S(1)} fusion(bf16[4,256,3328]{1,2,0:T(8,128)(2,1)S(1)} %fusion.2, bf16[256,4,64]{2,0,1:T(8,128)(2,1)S(1)} %get-tuple-element.18, bf16[256,4,64]{2,0,1:T(8,128)(2,1)S(1)} %get-tuple-element.17), kind=kOutput, calls=%fused_computation.14 | convolution fusion | flops 873365504 | bytes 7929856 | tf_op jit(solution)/shard_map/gts,tgd->sd/dot_general | solution.py:45
  54.8 1.4 fusion.13
  56.3 1.7 copy.82
  58.1 1.4 fusion.10
  59.5 1.1 fusion.64
  60.6 1.3 copy.84
  62.1 1.4 bitcast_convert_fusion
  63.5 2.0 %copy.85 = f32[8,256,256]{1,2,0:T(8,128)} copy(f32[8,256,256]{2,1,0:T(8,128)S(1)} %bitcast_convert_fusion) | data formatting | bytes 4194304 | tf_op jit(solution)/shard_map/convert_element_type | solution.py:101
  65.5 6.0 %convolution_bitcast_fusion.2 = f32[256,4,128]{2,0,1:T(8,128)S(1)} fusion(bf16[4,256,3328]{1,2,0:T(8,128)(2,1)} %copy-done.1, bf16[3328,256]{1,0:T(8,128)(2,1)} %bitcast.139), kind=kOutput, calls=%fused_computation.48 | convolution fusion | flops 872415232 | bytes 8192000 | tf_op jit(solution)/shard_map/gts,sd->tgd/dot_general | solution.py:45
  72.1 3.2 %add_convert_fusion = bf16[8,256,256]{1,2,0:T(8,128)(2,1)} fusion(f32[8,256,256]{1,2,0:T(8,128)} %copy.85, bf16[8,256,256]{1,2,0:T(8,128)(2,1)} %collective-permute-done.1), kind=kLoop, calls=%fused_computation.39 | loop fusion | flops 1572864 | bytes 4194304 | tf_op jit(solution)/shard_map/convert_element_type | solution.py:101
  75.3 4.2 %all-to-all-start.1 = ((bf16[8,256,256]{1,2,0:T(8,128)(2,1)}), bf16[8,256,256]{1,2,0:T(8,128)(2,1)}, u32[]{:S(2)}, u32[]{:S(2)}) async-start(bf16[8,256,256]{1,2,0:T(8,128)(2,1)} %add_convert_fusion), calls=%async_computation.1 | async-start | bytes 2097152 | tf_op jit(solution)/shard_map/all_to_all | solution.py:105
  81.1 2.4 %fusion.8 = bf16[8,256,512]{1,2,0:T(8,128)(2,1)} fusion(f32[512,8,256]{2,0,1:T(8,128)S(1)} %fusion.22, f32[512,8,256]{2,0,1:T(8,128)S(1)} %fusion.20, pred[]{:T(512)S(6)} %eq.63), kind=kLoop, calls=%fused_computation.29 | loop fusion | flops 1048576 | bytes 10485761 | tf_op jit(solution)/shard_map/convert_element_type | solution.py:100
  84.6 11.0 %all-to-all-done.1 = bf16[8,256,256]{1,2,0:T(8,128)(2,1)} async-done(((bf16[8,256,256]{1,2,0:T(8,128)(2,1)}), bf16[8,256,256]{1,2,0:T(8,128)(2,1)}, u32[]{:S(2)}, u32[]{:S(2)}) %all-to-all-start.1) | async-done | bytes 1048608 | tf_op jit(solution)/shard_map/all_to_all | solution.py:105
  95.5 1.4 convert_reduce_fusion.2
  98.1 1.1 copy-done.6
  99.1 1.3 convolution_add_fusion
  101.2 1.5 copy.115
  102.7 4.8 %all-to-all-start.2 = ((bf16[256,8,512]{2,0,1:T(8,128)(2,1)}), bf16[256,8,512]{2,0,1:T(8,128)(2,1)}, u32[]{:S(2)}, u32[]{:S(2)}) async-start(bf16[256,8,512]{2,0,1:T(8,128)(2,1)} %bitcast.131), calls=%async_computation.2 | async-start | bytes 4194304 | tf_op jit(solution)/shard_map/all_to_all | solution.py:204
  109.0 2.6 %collective-permute-done.3 = bf16[8,256,256]{1,2,0:T(8,128)(2,1)S(1)} collective-permute-done((bf16[8,256,256]{1,2,0:T(8,128)(2,1)S(1)}, bf16[8,256,256]{1,2,0:T(8,128)(2,1)S(1)}, u32[]{:S(2)}, u32[]{:S(2)}) %collective-permute-start.3) | collective-permute-done | bytes 1048608 | tf_op jit(solution)/shard_map/ppermute | solution.py:100
  111.6 1.4 fusion.12
  113.1 20.1 %all-to-all-done.2 = bf16[256,8,512]{2,0,1:T(8,128)(2,1)} async-done(((bf16[256,8,512]{2,0,1:T(8,128)(2,1)}), bf16[256,8,512]{2,0,1:T(8,128)(2,1)}, u32[]{:S(2)}, u32[]{:S(2)}) %all-to-all-start.2) | async-done | bytes 2097184 | tf_op jit(solution)/shard_map/all_to_all | solution.py:204
  133.1 5.8 %all-to-all-start.4 = ((bf16[8,256,256]{1,2,0:T(8,128)(2,1)}), bf16[8,256,256]{1,2,0:T(8,128)(2,1)S(1)}, u32[]{:S(2)}, u32[]{:S(2)}) async-start(bf16[8,256,256]{1,2,0:T(8,128)(2,1)} %fusion.12), calls=%async_computation.4 | async-start | bytes 2097152 | tf_op jit(solution)/shard_map/all_to_all | solution.py:105
  138.9 4.9 %fusion.7 = bf16[8,256,512]{1,2,0:T(8,128)(2,1)} fusion(bf16[8,256,512]{1,2,0:T(8,128)(2,1)} %collective-permute-done.2, f32[512,8,256]{2,0,1:T(8,128)} %copy-done.2, f32[512,8,256]{2,0,1:T(8,128)} %copy-done.3, pred[]{:T(512)S(6)} %eq.63), kind=kLoop, calls=%fused_computation.25 | loop fusion | flops 4194304 | bytes 12582913 | tf_op jit(solution)/shard_map/convert_element_type | solution.py:101
  143.9 10.8 %all-to-all-done.4 = bf16[8,256,256]{1,2,0:T(8,128)(2,1)S(1)} async-done(((bf16[8,256,256]{1,2,0:T(8,128)(2,1)}), bf16[8,256,256]{1,2,0:T(8,128)(2,1)S(1)}, u32[]{:S(2)}, u32[]{:S(2)}) %all-to-all-start.4) | async-done | bytes 1048608 | tf_op jit(solution)/shard_map/all_to_all | solution.py:105
  154.6 1.0 copy-done.9
  155.6 4.1 %all-to-all-start.3 = ((bf16[8,256,512]{1,2,0:T(8,128)(2,1)}), bf16[8,256,512]{1,2,0:T(8,128)(2,1)S(1)}, u32[]{:S(2)}, u32[]{:S(2)}) async-start(bf16[8,256,512]{1,2,0:T(8,128)(2,1)} %fusion.7), calls=%async_computation.3 | async-start | bytes 4194304 | tf_op jit(solution)/shard_map/all_to_all | solution.py:105
  159.7 2.7 %reduce_sum.60 = bf16[256,512]{1,0:T(8,128)(2,1)} reduce(bf16[256,8,512]{2,0,1:T(8,128)(2,1)} %all-to-all-done.2, bf16[]{:T(256)} %constant.216.clone.1), dimensions={1}, to_apply=%region_4.6 | reduce | flops 917504 | bytes 2359298 | tf_op jit(solution)/shard_map/reduce_sum | solution.py:205
  162.4 1.4 convert_reduce_fusion.1
  165.3 21.0 %all-to-all-done.3 = bf16[8,256,512]{1,2,0:T(8,128)(2,1)S(1)} async-done(((bf16[8,256,512]{1,2,0:T(8,128)(2,1)}), bf16[8,256,512]{1,2,0:T(8,128)(2,1)S(1)}, u32[]{:S(2)}, u32[]{:S(2)}) %all-to-all-start.3) | async-done | bytes 2097184 | tf_op jit(solution)/shard_map/all_to_all | solution.py:105
  186.3 1.1 convert_reduce_fusion
  187.4 2.0 %copy.90 = f32[256,512]{1,0:T(8,128)} copy(f32[256,512]{0,1:T(8,128)} %convert_reduce_fusion) | data formatting | bytes 1048576
  (86 shorter events, 12.9 us)
Async XLA Ops:
  0.6 1.2 copy-start
  0.6 3.7 %copy-start.4 = (bf16[256,4096]{1,0:T(8,128)(2,1)S(1)}, bf16[256,4096]{1,0:T(8,128)(2,1)}, u32[]{:S(2)}) copy-start(bf16[256,4096]{1,0:T(8,128)(2,1)} %param.9) | copy-start | bytes 6291460
  0.7 3.7 %copy-start.7 = (bf16[4096,128]{1,0:T(8,128)(2,1)S(1)}, bf16[4096,128]{1,0:T(8,128)(2,1)}, u32[]{:S(2)}) copy-start(bf16[4096,128]{1,0:T(8,128)(2,1)} %param.12) | copy-start | bytes 3145732
  6.7 10.7 %copy-start.15 = (s32[2,32]{1,0:T(2,128)S(1)}, s32[2,32]{1,0:T(2,128)}, u32[]{:S(2)}) copy-start(s32[2,32]{1,0:T(2,128)} %param.14) | copy-start | bytes 772
  6.7 23.9 %all-to-all-start = ((bf16[8,256,256]{2,1,0:T(8,128)(2,1)}), bf16[8,256,256]{2,1,0:T(8,128)(2,1)}, u32[]{:S(2)}, u32[]{:S(2)}) async-start(bf16[8,256,256]{2,1,0:T(8,128)(2,1)} %broadcast_in_dim.111), calls=%async_computation | async-start | bytes 2097152 | tf_op jit(solution)/shard_map/all_to_all | solution.py:93
  18.4 5.5 %copy-start.14 = (bf16[256,512]{1,0:T(8,128)(2,1)S(1)}, bf16[256,512]{1,0:T(8,128)(2,1)}, u32[]{:S(2)}) copy-start(bf16[256,512]{1,0:T(8,128)(2,1)} %param.15) | copy-start | bytes 786436
  30.7 2.9 %collective-permute-start = (bf16[8,256,256]{2,1,0:T(8,128)(2,1)}, bf16[8,256,256]{2,1,0:T(8,128)(2,1)S(1)}, u32[]{:S(2)}, u32[]{:S(2)}) collective-permute-start(bf16[8,256,256]{2,1,0:T(8,128)(2,1)} %all-to-all-done), channel_id=1, source_target_pairs={{0,8},{8,0},{1,9},{9,1},{2,10},{10,2},{3,11},{11,3},{4,12},{12,4},... | collective-permute-start | bytes 3145736 | tf_op jit(solution)/shard_map/ppermute | solution.py:94
  33.5 2.2 %copy-start.12 = (pred[256,3328]{0,1:T(8,128)(4,1)S(1)}, pred[256,3328]{0,1:T(8,128)(4,1)}, u32[]{:S(2)}) copy-start(pred[256,3328]{0,1:T(8,128)(4,1)} %bitcast_and_fusion) | copy-start | bytes 2555908
  35.7 2.5 %copy-start.10 = (bf16[13,256,256]{2,1,0:T(8,128)(2,1)}, bf16[13,256,256]{2,1,0:T(8,128)(2,1)S(1)}, u32[]{:S(2)}) copy-start(bf16[13,256,256]{2,1,0:T(8,128)(2,1)S(1)} %pad_maximum_fusion) | copy-start | bytes 5111812
  40.0 4.2 %copy-start.11 = (bf16[13,256,256]{2,1,0:T(8,128)(2,1)S(1)}, bf16[13,256,256]{2,1,0:T(8,128)(2,1)}, u32[]{:S(2)}) copy-start(bf16[13,256,256]{2,1,0:T(8,128)(2,1)} %copy-done.10) | copy-start | bytes 5111812
  40.0 4.2 %copy-start.13 = (pred[256,3328]{0,1:T(8,128)(4,1)S(1)}, pred[256,3328]{0,1:T(8,128)(4,1)}, u32[]{:S(2)}) copy-start(pred[256,3328]{0,1:T(8,128)(4,1)} %bitcast_and_fusion) | copy-start | bytes 2555908
  51.9 2.8 %copy-start.1 = (bf16[4,256,3328]{1,2,0:T(8,128)(2,1)}, bf16[4,256,3328]{1,2,0:T(8,128)(2,1)S(1)}, u32[]{:S(2)}) copy-start(bf16[4,256,3328]{1,2,0:T(8,128)(2,1)S(1)} %fusion.2) | copy-start | bytes 20447236
  61.9 10.1 %collective-permute-start.1 = (bf16[8,256,256]{1,2,0:T(8,128)(2,1)}, bf16[8,256,256]{1,2,0:T(8,128)(2,1)}, u32[]{:S(2)}, u32[]{:S(2)}) collective-permute-start(bf16[8,256,256]{1,2,0:T(8,128)(2,1)} %copy.84), channel_id=1, source_target_pairs={{0,8},{8,0},{1,9},{9,1},{2,10},{10,2},{3,11},{11,3},{4,12},{12,4},... | collective-permute-start | bytes 3145736 | tf_op jit(solution)/shard_map/ppermute | solution.py:100
  72.1 7.5 %copy-start.5 = (bf16[256,4096]{0,1:T(8,128)(2,1)S(1)}, bf16[256,4096]{0,1:T(8,128)(2,1)}, u32[]{:S(2)}) copy-start(bf16[256,4096]{0,1:T(8,128)(2,1)} %copy.87) | copy-start | bytes 6291460
  75.3 20.2 %all-to-all-start.1 = ((bf16[8,256,256]{1,2,0:T(8,128)(2,1)}), bf16[8,256,256]{1,2,0:T(8,128)(2,1)}, u32[]{:S(2)}, u32[]{:S(2)}) async-start(bf16[8,256,256]{1,2,0:T(8,128)(2,1)} %add_convert_fusion), calls=%async_computation.1 | async-start | bytes 2097152 | tf_op jit(solution)/shard_map/all_to_all | solution.py:105
  80.3 3.2 %copy-start.2 = (f32[512,8,256]{2,0,1:T(8,128)}, f32[512,8,256]{2,0,1:T(8,128)S(1)}, u32[]{:S(2)}) copy-start(f32[512,8,256]{2,0,1:T(8,128)S(1)} %fusion.20) | copy-start | bytes 12582916
  81.1 3.1 %copy-start.3 = (f32[512,8,256]{2,0,1:T(8,128)}, f32[512,8,256]{2,0,1:T(8,128)S(1)}, u32[]{:S(2)}) copy-start(f32[512,8,256]{2,0,1:T(8,128)S(1)} %fusion.22) | copy-start | bytes 12582916
  84.2 54.7 %collective-permute-start.2 = (bf16[8,256,512]{1,2,0:T(8,128)(2,1)}, bf16[8,256,512]{1,2,0:T(8,128)(2,1)}, u32[]{:S(2)}, u32[]{:S(2)}) collective-permute-start(bf16[8,256,512]{1,2,0:T(8,128)(2,1)} %fusion.8), channel_id=1, source_target_pairs={{0,8},{8,0},{1,9},{9,1},{2,10},{10,2},{3,11},{11,3},{4,12},{12,4},... | collective-permute-start | bytes 6291464 | tf_op jit(solution)/shard_map/ppermute | solution.py:100
  96.9 2.2 %copy-start.6 = (bf16[4096,512]{1,0:T(8,128)(2,1)S(1)}, bf16[4096,512]{1,0:T(8,128)(2,1)}, u32[]{:S(2)}) copy-start(bf16[4096,512]{1,0:T(8,128)(2,1)} %param.10) | copy-start | bytes 12582916
  99.1 1.4 copy-start.8
  102.7 30.4 %all-to-all-start.2 = ((bf16[256,8,512]{2,0,1:T(8,128)(2,1)}), bf16[256,8,512]{2,0,1:T(8,128)(2,1)}, u32[]{:S(2)}, u32[]{:S(2)}) async-start(bf16[256,8,512]{2,0,1:T(8,128)(2,1)} %bitcast.131), calls=%async_computation.2 | async-start | bytes 4194304 | tf_op jit(solution)/shard_map/all_to_all | solution.py:204
  108.9 2.7 %collective-permute-start.3 = (bf16[8,256,256]{1,2,0:T(8,128)(2,1)S(1)}, bf16[8,256,256]{1,2,0:T(8,128)(2,1)S(1)}, u32[]{:S(2)}, u32[]{:S(2)}) collective-permute-start(bf16[8,256,256]{1,2,0:T(8,128)(2,1)S(1)} %fusion.18), channel_id=1, source_target_pairs={{0,8},{8,0},{1,9},{9,1},{2,10},{10,2},{3,11},{11,3},{4,12},{12,4},... | collective-permute-start | bytes 3145736 | tf_op jit(solution)/shard_map/ppermute | solution.py:100
  133.1 21.5 %all-to-all-start.4 = ((bf16[8,256,256]{1,2,0:T(8,128)(2,1)}), bf16[8,256,256]{1,2,0:T(8,128)(2,1)S(1)}, u32[]{:S(2)}, u32[]{:S(2)}) async-start(bf16[8,256,256]{1,2,0:T(8,128)(2,1)} %fusion.12), calls=%async_computation.4 | async-start | bytes 2097152 | tf_op jit(solution)/shard_map/all_to_all | solution.py:105
  154.6 1.0 copy-start.9
  155.6 30.7 %all-to-all-start.3 = ((bf16[8,256,512]{1,2,0:T(8,128)(2,1)}), bf16[8,256,512]{1,2,0:T(8,128)(2,1)S(1)}, u32[]{:S(2)}, u32[]{:S(2)}) async-start(bf16[8,256,512]{1,2,0:T(8,128)(2,1)} %fusion.7), calls=%async_computation.3 | async-start | bytes 4194304 | tf_op jit(solution)/shard_map/all_to_all | solution.py:105
